TPU v7x, 128 devices: a whole 4x4x4 slice. The times are simulated.
128 devices in a mesh: dp: 32 (over y, x, core), proto: 4 (over z).
Axes of the slice: x: 4, y: 4, z: 4, core: 2. Of those that a mesh axis runs over, the one named last changes fastest.
Arguments:
- features: bfloat16 [16384, 2048], P('dp', 'proto'), may hold values from -8 to 8
- head_weight: bfloat16 [2048, 256], P('proto'), may hold values from -1 to 1
- prototypes: bfloat16 [256, 32768], P(None, 'proto'), may hold values from -1 to 1
Outputs:
- codes: bfloat16 [16384, 32768], P('dp', 'proto')
- proto_grad: float32 [256, 32768], P('dp', 'proto')
- head_grad: float32 [256, 2048], P('dp', 'proto')
All inputs are finite; a program needn't handle non-finite values.
Results may differ from a plain program's by a relative error of at most 0.009.
Values may be sent and summed in bfloat16 or wider, within the bound.
No kernel may reach another device: no remote copies, remote signals or barrier semaphores. Data moves between devices by JAX's collectives and lax.ppermute only.
A program may use at most 128 MiB of HBM per device.

v0:
```python
import math

import jax
import jax.numpy as jnp
from jax import lax
from jax.experimental import pallas as pl
from jax.experimental.pallas import tpu as pltpu
from jax.sharding import Mesh
from jax.sharding import PartitionSpec as P

PROTOS = 32768
ITERS = 3


soft_temp = 0.1

DP = ("y", "x", "core")
SIZES = {"y": 4, "x": 4, "core": 2, "z": 4}
F32 = jnp.float32
BF16 = jnp.bfloat16


def _shift(v, ax, k):
    n = SIZES[ax]
    return lax.ppermute(v, ax, [(i, (i + k) % n) for i in range(n)])


def _allsum(v, ax, dt=None):
    sent = v if dt is None else v.astype(dt)
    acc = v
    for k in range(1, SIZES[ax]):
        acc = acc + _shift(sent, ax, k).astype(v.dtype)
    return acc


def _allsum_dp(v):
    for ax in ("core", "x", "y"):
        v = _allsum(v, ax)
    return v


def _rs(a, ax, axis, dt=None):
    n = SIZES[ax]
    i = lax.axis_index(ax)
    acc = lax.dynamic_index_in_dim(a, i, axis, keepdims=False)
    for k in range(1, n):
        blk = lax.dynamic_index_in_dim(a, (i + k) % n, axis, keepdims=False)
        if dt is not None:
            blk = blk.astype(dt)
        acc = acc + _shift(blk, ax, k).astype(a.dtype)
    return acc


def _ag(v, ax):
    n = SIZES[ax]
    i = lax.axis_index(ax)
    parts = [v] + [_shift(v, ax, k) for k in range(1, n)]
    rel = jnp.stack(parts)
    idx = (i - jnp.arange(n)) % n
    return rel[idx]


def _rs_dp(part, dt):
    R, N = part.shape
    a = part.reshape(SIZES["y"], SIZES["x"], SIZES["core"], R // 32, N)
    a = _rs(a, "core", 2, dt)
    a = _rs(a, "x", 1, dt)
    a = _rs(a, "y", 0, dt)
    return a


def _score_kernel(u_ref, n_ref, s_ref, k_ref, col_ref, rs_ref):
    j = pl.program_id(0)
    sc = jnp.dot(u_ref[...], n_ref[...], preferred_element_type=F32)
    s = jnp.exp(sc * (1.0 / soft_temp))
    s_ref[...] = s
    k = s * s
    k_ref[:, pl.ds(pl.multiple_of(j * s.shape[1], s.shape[1]), s.shape[1])] = k.astype(BF16)
    col_ref[...] = jnp.sum(k, axis=0, keepdims=True)

    @pl.when(j == 0)
    def _():
        rs_ref[...] = jnp.zeros_like(rs_ref)

    rs_ref[...] += jnp.sum(s, axis=1, keepdims=True)


def _scores(unit_b, normed, bp=1024):
    T, E = unit_b.shape
    Pn = normed.shape[1]
    soft, kb, col, rs = pl.pallas_call(
        _score_kernel,
        grid=(Pn // bp,),
        in_specs=[pl.BlockSpec((T, E), lambda j: (0, 0)), pl.BlockSpec((E, bp), lambda j: (0, j))],
        out_specs=[
            pl.BlockSpec((T, bp), lambda j: (0, j)),
            pl.BlockSpec(memory_space=pltpu.VMEM),
            pl.BlockSpec((1, bp), lambda j: (0, j)),
            pl.BlockSpec((T, 1), lambda j: (0, 0)),
        ],
        out_shape=[
            jax.ShapeDtypeStruct((T, Pn), F32),
            jax.ShapeDtypeStruct((T, Pn), BF16),
            jax.ShapeDtypeStruct((1, Pn), F32),
            jax.ShapeDtypeStruct((T, 1), F32),
        ],
    )(unit_b, normed)
    return soft, kb, col[0], rs[:, 0]


def _split(v):
    hi = v.astype(BF16)
    lo = (v - hi.astype(F32)).astype(BF16)
    return jnp.stack([hi, lo])


def _colpass(kern_b, r):
    out = jnp.dot(_split(r), kern_b, preferred_element_type=F32)
    return out[0] + out[1]


def _rowpass(kern_b, c):
    out = jnp.dot(kern_b, _split(c).T, preferred_element_type=F32)
    return out[:, 0] + out[:, 1]


def on_device(features, head_weight, prototypes):
    partial_proj = jnp.dot(features, head_weight, preferred_element_type=F32)
    T, E = partial_proj.shape
    nz = SIZES["z"]
    proj_blk = _rs(partial_proj.reshape(nz, T // nz, E), "z", 0)
    projected = _ag(proj_blk, "z").reshape(T, E)
    length = jnp.sqrt(jnp.sum(projected * projected, axis=1, keepdims=True) + 1e-06)
    unit = projected / length
    unit_b = unit.astype(BF16)
    proto_f = prototypes.astype(F32)
    normed = (proto_f / jnp.sqrt(jnp.sum(proto_f * proto_f, axis=0, keepdims=True) + 1e-06)).astype(BF16)
    soft, kern_b, col0, soft_local = _scores(unit_b, normed)
    kern = soft * soft
    c = 1.0 / _allsum_dp(col0)
    rowpart = _rowpass(kern_b, c)
    both = _allsum(jnp.stack([rowpart, soft_local]), "z")
    r, soft_total = 1.0 / both[0], both[1]

    def sinkhorn_step(_, cr):
        c, r = cr
        c = 1.0 / _allsum_dp(_colpass(kern_b, r))
        r = 1.0 / _allsum(_rowpass(kern_b, c), "z")
        return c, r

    c, r = lax.fori_loop(1, ITERS, sinkhorn_step, (c, r))
    plan = kern * c[None, :] * r[:, None]
    probs = soft / soft_total[:, None]
    codes = (PROTOS * plan).astype(BF16)
    tokens_all = 32 * T
    factor = PROTOS / (soft_temp * math.sqrt(tokens_all))
    dscore = ((probs - plan) * factor).astype(BF16)
    half = dscore.shape[1] // 2
    pg = []
    for h in range(2):
        pg_part = lax.dot_general(
            unit_b, dscore[:, h * half:(h + 1) * half], (((0,), (0,)), ((), ())), preferred_element_type=F32
        )
        pg.append(_rs_dp(pg_part, BF16))
    proto_grad = jnp.concatenate(pg, axis=1)
    dunit_part = lax.dot_general(dscore, normed, (((1,), (1,)), ((), ())), preferred_element_type=F32)
    dunit = _allsum(dunit_part, "z", BF16)
    dproj = ((dunit - unit * jnp.sum(unit * dunit, axis=1, keepdims=True)) / length).astype(BF16)
    head_part = lax.dot_general(dproj, features, (((0,), (0,)), ((), ())), preferred_element_type=F32)
    head_grad = _rs_dp(head_part, BF16)
    return (codes, proto_grad, head_grad)


def solution(mesh):
    devs = mesh.devices.reshape(SIZES["y"], SIZES["x"], SIZES["core"], SIZES["z"])
    m4 = Mesh(devs, ("y", "x", "core", "z"))
    in_specs = (P(DP, "z"), P("z", None), P(None, "z"))
    out_specs = (P(DP, "z"), P(DP, "z"), P(DP, "z"))

    return jax.shard_map(on_device, mesh=m4, in_specs=in_specs, out_specs=out_specs, check_vma=False)
```

profile of v0, /device:TPU:6, one launch (start us, length us, event | category | flops | bytes accessed | tf_op | source)
XLA Modules:
  0.0 211.2 jit_solution(1077040586223243288)
XLA Ops:
  3.1 2.0 collective-permute-start.10
  5.1 3.6 %collective-permute-start.11 = (f32[128,256]{1,0:T(8,128)S(1)}, f32[128,256]{1,0:T(8,128)S(1)}, u32[]{:S(2)}, u32[]{:S(2)}) collective-permute-start(f32[128,256]{1,0:T(8,128)S(1)} %get-tuple-element.69), channel_id=1, source_target_pairs={{0,2},{1,3},{2,0},{3,1},{4,6},{5,7},{6,4},{7,5},{8,10},{9,11},{10,... | collective-permute-start | bytes 393224 | tf_op jit(solution)/shard_map/ppermute | solution.py:25
  9.7 3.1 %fusion.9 = f32[8192]{0:T(1024)S(1)} fusion(bf16[256,8192]{1,0:T(8,128)(2,1)} %param.7), kind=kLoop, calls=%fused_computation.23 | loop fusion | flops 6283264 | bytes 4227072 | tf_op jit(solution)/shard_map/reduce_sum | solution.py:137
  12.8 2.9 %fusion.10.n_ref = bf16[256,8192]{1,0:T(8,128)(2,1)} fusion(bf16[256,8192]{1,0:T(8,128)(2,1)S(1)} %copy-done.2, f32[8192]{0:T(1024)S(1)} %add_sqrt_fusion), kind=kLoop, calls=%fused_computation.24 | loop fusion | flops 6291456 | bytes 8421376 | tf_op jit(solution)/shard_map/convert_element_type | solution.py:137
  17.1 2.5 %collective-permute-start.15 = (f32[128,256]{1,0:T(8,128)S(1)}, f32[128,256]{1,0:T(8,128)S(1)}, u32[]{:S(2)}, u32[]{:S(2)}) collective-permute-start(f32[128,256]{1,0:T(8,128)S(1)} %fusion.34), channel_id=1, source_target_pairs={{0,3},{1,0},{2,1},{3,2},{4,7},{5,4},{6,5},{7,6},{8,11},{9,8},{10,9... | collective-permute-start | bytes 393224 | tf_op jit(solution)/shard_map/ppermute | solution.py:25
  19.6 3.8 %collective-permute-done.14 = f32[128,256]{1,0:T(8,128)S(1)} collective-permute-done((f32[128,256]{1,0:T(8,128)S(1)}, f32[128,256]{1,0:T(8,128)S(1)}, u32[]{:S(2)}, u32[]{:S(2)}) %collective-permute-start.14) | collective-permute-done | bytes 131104 | tf_op jit(solution)/shard_map/ppermute | solution.py:25
  23.5 2.2 %collective-permute-done.13 = f32[128,256]{1,0:T(8,128)S(1)} collective-permute-done((f32[128,256]{1,0:T(8,128)S(1)}, f32[128,256]{1,0:T(8,128)S(1)}, u32[]{:S(2)}, u32[]{:S(2)}) %collective-permute-start.13) | collective-permute-done | bytes 131104 | tf_op jit(solution)/shard_map/ppermute | solution.py:25
  27.4 13.6 %shard_map.58 = (f32[512,8192]{1,0:T(8,128)}, bf16[512,8192]{1,0:T(8,128)(2,1)}, f32[1,8192]{1,0:T(1,128)}, f32[512,1]{1,0:T(8,128)}) custom-call(bf16[512,256]{1,0:T(8,128)(2,1)} %get-tuple-element.51.u_ref, bf16[256,8192]{1,0:T(8,128)(2,1)} %fusion.10.n_ref), custom_call_target="tpu_custom_call" | custom-call | tf_op jit(solution)/shard_map/pallas_call | solution.py:91
  43.8 2.4 %collective-permute-start.18 = (f32[8192]{0:T(1024)S(1)}, f32[8192]{0:T(1024)S(1)}, u32[]{:S(2)}, u32[]{:S(2)}) collective-permute-start(f32[8192]{0:T(1024)S(1)} %add.392), channel_id=1, source_target_pairs={{0,16},{8,24},{16,0},{24,8},{1,17},{9,25},{17,1},{25,9},{2,18},{10... | collective-permute-start | bytes 98312 | tf_op jit(solution)/shard_map/ppermute | solution.py:25
  47.3 1.9 collective-permute-done.18
  49.2 2.1 %collective-permute-done.19 = f32[8192]{0:T(1024)S(1)} collective-permute-done((f32[8192]{0:T(1024)S(1)}, f32[8192]{0:T(1024)S(1)}, u32[]{:S(2)}, u32[]{:S(2)}) %collective-permute-start.19) | collective-permute-done | bytes 32800 | tf_op jit(solution)/shard_map/ppermute | solution.py:25
  51.3 1.6 collective-permute-start.20
  53.0 2.9 %collective-permute-start.21 = (f32[8192]{0:T(1024)S(1)}, f32[8192]{0:T(1024)S(1)}, u32[]{:S(2)}, u32[]{:S(2)}) collective-permute-start(f32[8192]{0:T(1024)S(1)} %add_add_fusion.1), channel_id=1, source_target_pairs={{0,64},{32,96},{64,0},{96,32},{1,65},{33,97},{65,1},{97,33},{2,66}... | collective-permute-start | bytes 98312 | tf_op jit(solution)/shard_map/ppermute | solution.py:25
  60.4 5.6 %fusion.46 = f32[512,2]{0,1:T(2,128)S(1)} fusion(bf16[512,8192]{1,0:T(8,128)(2,1)} %get-tuple-element.116, bf16[1,8192]{1,0:T(2,128)(2,1)S(1)} %stack.52, bf16[1,8192]{1,0:T(2,128)(2,1)S(1)} %stack.51), kind=kOutput, calls=%fused_computation.99 | convolution fusion | flops 16842752 | bytes 8425472 | tf_op jit(solution)/shard_map/dot_general | solution.py:123
  66.2 2.0 collective-permute-start.24
  69.6 1.4 collective-permute-done.23
  71.9 62.8 %while.12 = (s32[]{:T(128)}, f32[8192]{0:T(1024)}, f32[512]{0:T(512)S(1)}, bf16[512,8192]{1,0:T(8,128)(2,1)}, s32[]{:T(128)}) while((s32[]{:T(128)}, f32[8192]{0:T(1024)}, f32[512]{0:T(512)S(1)}, bf16[512,8192]{1,0:T(8,128)(2,1)}, s32[]{:T(128)}) %tuple.52), condition=%wide.region_3.4_spmd, body=%wide.region_2.3_spmd.sunk | while | flops 33735168 | bytes 52025832 | solution.py:151
  72.0 4.7 %fusion.82 = f32[2,8192]{1,0:T(2,128)S(1)} fusion(bf16[512,8192]{1,0:T(8,128)(2,1)} %get-tuple-element.126, bf16[1,512]{1,0:T(2,128)(2,1)S(1)} %stack.59, bf16[1,512]{1,0:T(2,128)(2,1)S(1)} %stack.60), kind=kOutput, calls=%fused_computation.10.clone.1 | convolution fusion | flops 16781312 | bytes 8456192 | tf_op jit(solution)/shard_map/while/body/eval_jaxpr/dot_general | solution.py:118
  78.1 2.0 collective-permute-start.2
  81.3 1.9 collective-permute-done.1
  84.4 2.6 %collective-permute-start.4 = (f32[8192]{0:T(1024)S(1)}, f32[8192]{0:T(1024)S(1)}, u32[]{:S(2)}, u32[]{:S(2)}) collective-permute-start(f32[8192]{0:T(1024)S(1)} %add_add_fusion.4), channel_id=1, source_target_pairs={{0,96},{32,0},{64,32},{96,64},{1,97},{33,1},{65,33},{97,65},{2,98}... | collective-permute-start | bytes 98312 | tf_op jit(solution)/shard_map/while/body/eval_jaxpr/ppermute | solution.py:25
  88.6 3.9 %collective-permute-done.5 = f32[8192]{0:T(1024)S(1)} collective-permute-done((f32[8192]{0:T(1024)S(1)}, f32[8192]{0:T(1024)S(1)}, u32[]{:S(2)}, u32[]{:S(2)}) %collective-permute-start.5) | collective-permute-done | bytes 32800 | tf_op jit(solution)/shard_map/while/body/eval_jaxpr/ppermute | solution.py:25
  93.2 2.3 %convolution_bitcast_fusion.2 = f32[512,2]{0,1:T(2,128)S(1)} fusion(bf16[512,8192]{1,0:T(8,128)(2,1)S(1)} %copy-done.1, bf16[1,8192]{1,0:T(2,128)(2,1)S(1)} %stack.61, bf16[1,8192]{1,0:T(2,128)(2,1)S(1)} %stack.62), kind=kOutput, calls=%fused_computation.1.clone.1 | convolution fusion | flops 16842752 | bytes 8425472 | tf_op jit(solution)/shard_map/while/body/eval_jaxpr/dot_general | solution.py:123
  95.5 2.7 %collective-permute-start.7 = (f32[512]{0:T(512)S(1)}, f32[512]{0:T(512)S(1)}, u32[]{:S(2)}, u32[]{:S(2)}) collective-permute-start(f32[512]{0:T(512)S(1)} %bitcast.169), channel_id=1, source_target_pairs={{0,3},{1,0},{2,1},{3,2},{4,7},{5,4},{6,5},{7,6},{8,11},{9,8},{10,9... | collective-permute-start | bytes 6152 | tf_op jit(solution)/shard_map/while/body/eval_jaxpr/ppermute | solution.py:25
  98.1 1.4 collective-permute-start.8
  99.5 3.7 %collective-permute-done.8 = f32[512]{0:T(512)S(1)} collective-permute-done((f32[512]{0:T(512)S(1)}, f32[512]{0:T(512)S(1)}, u32[]{:S(2)}, u32[]{:S(2)}) %collective-permute-start.8) | collective-permute-done | bytes 2080 | tf_op jit(solution)/shard_map/while/body/eval_jaxpr/ppermute | solution.py:25
  104.4 4.7 %fusion.82 = f32[2,8192]{1,0:T(2,128)S(1)} fusion(bf16[512,8192]{1,0:T(8,128)(2,1)} %get-tuple-element.126, bf16[1,512]{1,0:T(2,128)(2,1)S(1)} %stack.59, bf16[1,512]{1,0:T(2,128)(2,1)S(1)} %stack.60), kind=kOutput, calls=%fused_computation.10.clone.1 | convolution fusion | flops 16781312 | bytes 8456192 | tf_op jit(solution)/shard_map/while/body/eval_jaxpr/dot_general | solution.py:118
  110.4 1.7 collective-permute-start.1
  112.1 2.2 %collective-permute-start.2 = (f32[8192]{0:T(1024)S(1)}, f32[8192]{0:T(1024)S(1)}, u32[]{:S(2)}, u32[]{:S(2)}) collective-permute-start(f32[8192]{0:T(1024)S(1)} %add.597), channel_id=1, source_target_pairs={{0,16},{8,24},{16,0},{24,8},{1,17},{9,25},{17,1},{25,9},{2,18},{10... | collective-permute-start | bytes 98312 | tf_op jit(solution)/shard_map/while/body/eval_jaxpr/ppermute | solution.py:25
  115.6 2.0 collective-permute-done.2
  122.2 2.4 %collective-permute-done.5 = f32[8192]{0:T(1024)S(1)} collective-permute-done((f32[8192]{0:T(1024)S(1)}, f32[8192]{0:T(1024)S(1)}, u32[]{:S(2)}, u32[]{:S(2)}) %collective-permute-start.5) | collective-permute-done | bytes 32800 | tf_op jit(solution)/shard_map/while/body/eval_jaxpr/ppermute | solution.py:25
  126.1 2.3 %convolution_bitcast_fusion.2 = f32[512,2]{0,1:T(2,128)S(1)} fusion(bf16[512,8192]{1,0:T(8,128)(2,1)S(1)} %copy-done.1, bf16[1,8192]{1,0:T(2,128)(2,1)S(1)} %stack.61, bf16[1,8192]{1,0:T(2,128)(2,1)S(1)} %stack.62), kind=kOutput, calls=%fused_computation.1.clone.1 | convolution fusion | flops 16842752 | bytes 8425472 | tf_op jit(solution)/shard_map/while/body/eval_jaxpr/dot_general | solution.py:123
  132.0 1.6 collective-permute-done.8
  134.7 11.2 %multiply_convert_fusion = (bf16[512,8192]{1,0:T(8,128)(2,1)S(1)}, bf16[512,8192]{1,0:T(8,128)(2,1)}) fusion(f32[512,8192]{1,0:T(8,128)} %get-tuple-element.29, f32[512]{0:T(512)S(1)} %bitcast.181, f32[512]{0:T(512)S(1)} %get-tuple-element.34, f32[8192]{0:T(1024)} %get-tuple-element.33), kind=kLoop, calls=%fused_computation.18 | loop fusion | flops 37748736 | bytes 33591296 | tf_op jit(solution)/shard_map/convert_element_type | solution.py:157
  145.9 2.4 %fusion.61 = (bf16[512,256]{1,0:T(8,128)(2,1)S(1)}, f32[512,256]{1,0:T(8,128)S(1)}) fusion(bf16[512,8192]{1,0:T(8,128)(2,1)S(1)} %get-tuple-element.53, bf16[256,8192]{1,0:T(8,128)(2,1)S(1)} %copy-done.3), kind=kOutput, calls=%fused_computation.136 | convolution fusion | flops 2147614720 | bytes 13369344 | tf_op jit(solution)/shard_map/dot_general | solution.py:166
  149.2 2.6 %collective-permute-start.41 = (bf16[512,256]{1,0:T(8,128)(2,1)S(1)}, bf16[512,256]{1,0:T(8,128)(2,1)S(1)}, u32[]{:S(2)}, u32[]{:S(2)}) collective-permute-start(bf16[512,256]{1,0:T(8,128)(2,1)S(1)} %get-tuple-element.78), channel_id=1, source_target_pairs={{0,2},{1,3},{2,0},{3,1},{4,6},{5,7},{6,4},{7,5},{8,10},{9,11},{10,... | collective-permute-start | bytes 786440 | tf_op jit(solution)/shard_map/ppermute | solution.py:25
  153.5 3.0 %collective-permute-done.40 = bf16[512,256]{1,0:T(8,128)(2,1)S(1)} collective-permute-done((bf16[512,256]{1,0:T(8,128)(2,1)S(1)}, bf16[512,256]{1,0:T(8,128)(2,1)S(1)}, u32[]{:S(2)}, u32[]{:S(2)}) %collective-permute-start.40) | collective-permute-done | bytes 262176 | tf_op jit(solution)/shard_map/ppermute | solution.py:25
  156.4 2.8 %collective-permute-done.41 = bf16[512,256]{1,0:T(8,128)(2,1)S(1)} collective-permute-done((bf16[512,256]{1,0:T(8,128)(2,1)S(1)}, bf16[512,256]{1,0:T(8,128)(2,1)S(1)}, u32[]{:S(2)}, u32[]{:S(2)}) %collective-permute-start.41) | collective-permute-done | bytes 262176 | tf_op jit(solution)/shard_map/ppermute | solution.py:25
  162.3 2.3 %collective-permute-start.44 = (bf16[4,8,512]{2,1,0:T(8,128)(2,1)S(1)}, bf16[4,8,512]{2,1,0:T(8,128)(2,1)S(1)}, u32[]{:S(2)}, u32[]{:S(2)}) collective-permute-start(bf16[4,8,512]{2,1,0:T(8,128)(2,1)S(1)} %get-tuple-element.70), channel_id=1, source_target_pairs={{0,8},{8,16},{16,24},{24,0},{1,9},{9,17},{17,25},{25,1},{2,10},{10... | collective-permute-start | bytes 98312 | tf_op jit(solution)/shard_map/ppermute | solution.py:25
  166.9 3.2 %collective-permute-done.45 = bf16[4,8,512]{2,1,0:T(8,128)(2,1)S(1)} collective-permute-done((bf16[4,8,512]{2,1,0:T(8,128)(2,1)S(1)}, bf16[4,8,512]{2,1,0:T(8,128)(2,1)S(1)}, u32[]{:S(2)}, u32[]{:S(2)}) %collective-permute-start.45) | collective-permute-done | bytes 32800 | tf_op jit(solution)/shard_map/ppermute | solution.py:25
  170.7 2.4 %collective-permute-start.48 = (bf16[8,512]{1,0:T(8,128)(2,1)S(1)}, bf16[8,512]{1,0:T(8,128)(2,1)S(1)}, u32[]{:S(2)}, u32[]{:S(2)}) collective-permute-start(bf16[8,512]{1,0:T(8,128)(2,1)S(1)} %get-tuple-element.75), channel_id=1, source_target_pairs={{0,64},{32,96},{64,0},{96,32},{1,65},{33,97},{65,1},{97,33},{2,66}... | collective-permute-start | bytes 24584 | tf_op jit(solution)/shard_map/ppermute | solution.py:25
  181.6 2.0 collective-permute-start.34
  184.7 3.5 %collective-permute-done.27 = bf16[4,8,4096]{2,1,0:T(8,128)(2,1)S(1)} collective-permute-done((bf16[4,8,4096]{2,1,0:T(8,128)(2,1)S(1)}, bf16[4,8,4096]{2,1,0:T(8,128)(2,1)S(1)}, u32[]{:S(2)}, u32[]{:S(2)}) %collective-permute-start.27) | collective-permute-done | bytes 262176 | tf_op jit(solution)/shard_map/ppermute | solution.py:25
  189.4 6.5 %collective-permute-done.29 = bf16[4,8,4096]{2,1,0:T(8,128)(2,1)S(1)} collective-permute-done((bf16[4,8,4096]{2,1,0:T(8,128)(2,1)S(1)}, bf16[4,8,4096]{2,1,0:T(8,128)(2,1)S(1)}, u32[]{:S(2)}, u32[]{:S(2)}) %collective-permute-start.29) | collective-permute-done | bytes 262176 | tf_op jit(solution)/shard_map/ppermute | solution.py:25
  197.3 2.4 %collective-permute-start.31 = (bf16[8,4096]{1,0:T(8,128)(2,1)S(1)}, bf16[8,4096]{1,0:T(8,128)(2,1)S(1)}, u32[]{:S(2)}, u32[]{:S(2)}) collective-permute-start(bf16[8,4096]{1,0:T(8,128)(2,1)S(1)} %get-tuple-element.63), channel_id=1, source_target_pairs={{0,64},{32,96},{64,0},{96,32},{1,65},{33,97},{65,1},{97,33},{2,66}... | collective-permute-start | bytes 196616 | tf_op jit(solution)/shard_map/ppermute | solution.py:25
  200.3 2.7 %collective-permute-done.36 = bf16[4,8,4096]{2,1,0:T(8,128)(2,1)S(1)} collective-permute-done((bf16[4,8,4096]{2,1,0:T(8,128)(2,1)S(1)}, bf16[4,8,4096]{2,1,0:T(8,128)(2,1)S(1)}, u32[]{:S(2)}, u32[]{:S(2)}) %collective-permute-start.36) | collective-permute-done | bytes 262176 | tf_op jit(solution)/shard_map/ppermute | solution.py:25
  204.3 1.8 collective-permute-start.38
  206.2 2.0 collective-permute-start.39
  (162 shorter events, 63.6 us)
Async XLA Ops:
  3.1 12.6 %collective-permute-start.10 = (f32[128,256]{1,0:T(8,128)S(1)}, f32[128,256]{1,0:T(8,128)S(1)}, u32[]{:S(2)}, u32[]{:S(2)}) collective-permute-start(f32[128,256]{1,0:T(8,128)S(1)} %get-tuple-element.67), channel_id=1, source_target_pairs={{0,1},{1,2},{2,3},{3,0},{4,5},{5,6},{6,7},{7,4},{8,9},{9,10},{10,1... | collective-permute-start | bytes 393224 | tf_op jit(solution)/shard_map/ppermute | solution.py:25
  5.1 10.6 %collective-permute-start.11 = (f32[128,256]{1,0:T(8,128)S(1)}, f32[128,256]{1,0:T(8,128)S(1)}, u32[]{:S(2)}, u32[]{:S(2)}) collective-permute-start(f32[128,256]{1,0:T(8,128)S(1)} %get-tuple-element.69), channel_id=1, source_target_pairs={{0,2},{1,3},{2,0},{3,1},{4,6},{5,7},{6,4},{7,5},{8,10},{9,11},{10,... | collective-permute-start | bytes 393224 | tf_op jit(solution)/shard_map/ppermute | solution.py:25
  8.7 7.1 %collective-permute-start.12 = (f32[128,256]{1,0:T(8,128)S(1)}, f32[128,256]{1,0:T(8,128)S(1)}, u32[]{:S(2)}, u32[]{:S(2)}) collective-permute-start(f32[128,256]{1,0:T(8,128)S(1)} %get-tuple-element.68), channel_id=1, source_target_pairs={{0,3},{1,0},{2,1},{3,2},{4,7},{5,4},{6,5},{7,6},{8,11},{9,8},{10,9... | collective-permute-start | bytes 393224 | tf_op jit(solution)/shard_map/ppermute | solution.py:25
  15.8 7.6 %collective-permute-start.14 = (f32[128,256]{1,0:T(8,128)S(1)}, f32[128,256]{1,0:T(8,128)S(1)}, u32[]{:S(2)}, u32[]{:S(2)}) collective-permute-start(f32[128,256]{1,0:T(8,128)S(1)} %fusion.34), channel_id=1, source_target_pairs={{0,2},{1,3},{2,0},{3,1},{4,6},{5,7},{6,4},{7,5},{8,10},{9,11},{10,... | collective-permute-start | bytes 393224 | tf_op jit(solution)/shard_map/ppermute | solution.py:25
  17.1 6.4 %collective-permute-start.15 = (f32[128,256]{1,0:T(8,128)S(1)}, f32[128,256]{1,0:T(8,128)S(1)}, u32[]{:S(2)}, u32[]{:S(2)}) collective-permute-start(f32[128,256]{1,0:T(8,128)S(1)} %fusion.34), channel_id=1, source_target_pairs={{0,3},{1,0},{2,1},{3,2},{4,7},{5,4},{6,5},{7,6},{8,11},{9,8},{10,9... | collective-permute-start | bytes 393224 | tf_op jit(solution)/shard_map/ppermute | solution.py:25
  19.6 6.2 %collective-permute-start.13 = (f32[128,256]{1,0:T(8,128)S(1)}, f32[128,256]{1,0:T(8,128)S(1)}, u32[]{:S(2)}, u32[]{:S(2)}) collective-permute-start(f32[128,256]{1,0:T(8,128)S(1)} %fusion.34), channel_id=1, source_target_pairs={{0,1},{1,2},{2,3},{3,0},{4,5},{5,6},{6,7},{7,4},{8,9},{9,10},{10,1... | collective-permute-start | bytes 393224 | tf_op jit(solution)/shard_map/ppermute | solution.py:25
  43.8 5.4 %collective-permute-start.18 = (f32[8192]{0:T(1024)S(1)}, f32[8192]{0:T(1024)S(1)}, u32[]{:S(2)}, u32[]{:S(2)}) collective-permute-start(f32[8192]{0:T(1024)S(1)} %add.392), channel_id=1, source_target_pairs={{0,16},{8,24},{16,0},{24,8},{1,17},{9,25},{17,1},{25,9},{2,18},{10... | collective-permute-start | bytes 98312 | tf_op jit(solution)/shard_map/ppermute | solution.py:25
  46.2 5.1 %collective-permute-start.19 = (f32[8192]{0:T(1024)S(1)}, f32[8192]{0:T(1024)S(1)}, u32[]{:S(2)}, u32[]{:S(2)}) collective-permute-start(f32[8192]{0:T(1024)S(1)} %add.392), channel_id=1, source_target_pairs={{0,24},{8,0},{16,8},{24,16},{1,25},{9,1},{17,9},{25,17},{2,26},{10... | collective-permute-start | bytes 98312 | tf_op jit(solution)/shard_map/ppermute | solution.py:25
  51.3 7.0 %collective-permute-start.20 = (f32[8192]{0:T(1024)S(1)}, f32[8192]{0:T(1024)S(1)}, u32[]{:S(2)}, u32[]{:S(2)}) collective-permute-start(f32[8192]{0:T(1024)S(1)} %add_add_fusion.1), channel_id=1, source_target_pairs={{0,32},{32,64},{64,96},{96,0},{1,33},{33,65},{65,97},{97,1},{2,34}... | collective-permute-start | bytes 98312 | tf_op jit(solution)/shard_map/ppermute | solution.py:25
  53.0 5.4 %collective-permute-start.21 = (f32[8192]{0:T(1024)S(1)}, f32[8192]{0:T(1024)S(1)}, u32[]{:S(2)}, u32[]{:S(2)}) collective-permute-start(f32[8192]{0:T(1024)S(1)} %add_add_fusion.1), channel_id=1, source_target_pairs={{0,64},{32,96},{64,0},{96,32},{1,65},{33,97},{65,1},{97,33},{2,66}... | collective-permute-start | bytes 98312 | tf_op jit(solution)/shard_map/ppermute | solution.py:25
  66.1 4.9 %collective-permute-start.23 = (f32[2,512]{1,0:T(2,128)S(1)}, f32[2,512]{1,0:T(2,128)S(1)}, u32[]{:S(2)}, u32[]{:S(2)}) collective-permute-start(f32[2,512]{1,0:T(2,128)S(1)} %pad_maximum_fusion.2), channel_id=1, source_target_pairs={{0,1},{1,2},{2,3},{3,0},{4,5},{5,6},{6,7},{7,4},{8,9},{9,10},{10,1... | collective-permute-start | bytes 12296 | tf_op jit(solution)/shard_map/ppermute | solution.py:25
  66.2 5.2 %collective-permute-start.24 = (f32[2,512]{1,0:T(2,128)S(1)}, f32[2,512]{1,0:T(2,128)S(1)}, u32[]{:S(2)}, u32[]{:S(2)}) collective-permute-start(f32[2,512]{1,0:T(2,128)S(1)} %pad_maximum_fusion.2), channel_id=1, source_target_pairs={{0,2},{1,3},{2,0},{3,1},{4,6},{5,7},{6,4},{7,5},{8,10},{9,11},{10,... | collective-permute-start | bytes 12296 | tf_op jit(solution)/shard_map/ppermute | solution.py:25
  78.1 5.1 %collective-permute-start.1 = (f32[8192]{0:T(1024)S(1)}, f32[8192]{0:T(1024)S(1)}, u32[]{:S(2)}, u32[]{:S(2)}) collective-permute-start(f32[8192]{0:T(1024)S(1)} %add.597), channel_id=1, source_target_pairs={{0,24},{8,0},{16,8},{24,16},{1,25},{9,1},{17,9},{25,17},{2,26},{10... | collective-permute-start | bytes 98312 | tf_op jit(solution)/shard_map/while/body/eval_jaxpr/ppermute | solution.py:25
  78.1 5.5 %collective-permute-start.2 = (f32[8192]{0:T(1024)S(1)}, f32[8192]{0:T(1024)S(1)}, u32[]{:S(2)}, u32[]{:S(2)}) collective-permute-start(f32[8192]{0:T(1024)S(1)} %add.597), channel_id=1, source_target_pairs={{0,16},{8,24},{16,0},{24,8},{1,17},{9,25},{17,1},{25,9},{2,18},{10... | collective-permute-start | bytes 98312 | tf_op jit(solution)/shard_map/while/body/eval_jaxpr/ppermute | solution.py:25
  80.1 4.3 %collective-permute-start.3 = (f32[8192]{0:T(1024)S(1)}, f32[8192]{0:T(1024)S(1)}, u32[]{:S(2)}, u32[]{:S(2)}) collective-permute-start(f32[8192]{0:T(1024)S(1)} %add.597), channel_id=1, source_target_pairs={{0,8},{8,16},{16,24},{24,0},{1,9},{9,17},{17,25},{25,1},{2,10},{10... | collective-permute-start | bytes 98312 | tf_op jit(solution)/shard_map/while/body/eval_jaxpr/ppermute | solution.py:25
  84.4 4.2 %collective-permute-start.4 = (f32[8192]{0:T(1024)S(1)}, f32[8192]{0:T(1024)S(1)}, u32[]{:S(2)}, u32[]{:S(2)}) collective-permute-start(f32[8192]{0:T(1024)S(1)} %add_add_fusion.4), channel_id=1, source_target_pairs={{0,96},{32,0},{64,32},{96,64},{1,97},{33,1},{65,33},{97,65},{2,98}... | collective-permute-start | bytes 98312 | tf_op jit(solution)/shard_map/while/body/eval_jaxpr/ppermute | solution.py:25
  87.0 5.5 %collective-permute-start.5 = (f32[8192]{0:T(1024)S(1)}, f32[8192]{0:T(1024)S(1)}, u32[]{:S(2)}, u32[]{:S(2)}) collective-permute-start(f32[8192]{0:T(1024)S(1)} %add_add_fusion.4), channel_id=1, source_target_pairs={{0,64},{32,96},{64,0},{96,32},{1,65},{33,97},{65,1},{97,33},{2,66}... | collective-permute-start | bytes 98312 | tf_op jit(solution)/shard_map/while/body/eval_jaxpr/ppermute | solution.py:25
  87.0 5.5 %collective-permute-start.6 = (f32[8192]{0:T(1024)S(1)}, f32[8192]{0:T(1024)S(1)}, u32[]{:S(2)}, u32[]{:S(2)}) collective-permute-start(f32[8192]{0:T(1024)S(1)} %add_add_fusion.4), channel_id=1, source_target_pairs={{0,32},{32,64},{64,96},{96,0},{1,33},{33,65},{65,97},{97,1},{2,34}... | collective-permute-start | bytes 98312 | tf_op jit(solution)/shard_map/while/body/eval_jaxpr/ppermute | solution.py:25
  98.1 5.1 %collective-permute-start.8 = (f32[512]{0:T(512)S(1)}, f32[512]{0:T(512)S(1)}, u32[]{:S(2)}, u32[]{:S(2)}) collective-permute-start(f32[512]{0:T(512)S(1)} %bitcast.170), channel_id=1, source_target_pairs={{0,2},{1,3},{2,0},{3,1},{4,6},{5,7},{6,4},{7,5},{8,10},{9,11},{10,... | collective-permute-start | bytes 6152 | tf_op jit(solution)/shard_map/while/body/eval_jaxpr/ppermute | solution.py:25
  99.5 4.8 %collective-permute-start.9 = (f32[512]{0:T(512)S(1)}, f32[512]{0:T(512)S(1)}, u32[]{:S(2)}, u32[]{:S(2)}) collective-permute-start(f32[512]{0:T(512)S(1)} %bitcast.171), channel_id=1, source_target_pairs={{0,1},{1,2},{2,3},{3,0},{4,5},{5,6},{6,7},{7,4},{8,9},{9,10},{10,1... | collective-permute-start | bytes 6152 | tf_op jit(solution)/shard_map/while/body/eval_jaxpr/ppermute | solution.py:25
  110.4 5.1 %collective-permute-start.1 = (f32[8192]{0:T(1024)S(1)}, f32[8192]{0:T(1024)S(1)}, u32[]{:S(2)}, u32[]{:S(2)}) collective-permute-start(f32[8192]{0:T(1024)S(1)} %add.597), channel_id=1, source_target_pairs={{0,24},{8,0},{16,8},{24,16},{1,25},{9,1},{17,9},{25,17},{2,26},{10... | collective-permute-start | bytes 98312 | tf_op jit(solution)/shard_map/while/body/eval_jaxpr/ppermute | solution.py:25
  112.1 5.4 %collective-permute-start.2 = (f32[8192]{0:T(1024)S(1)}, f32[8192]{0:T(1024)S(1)}, u32[]{:S(2)}, u32[]{:S(2)}) collective-permute-start(f32[8192]{0:T(1024)S(1)} %add.597), channel_id=1, source_target_pairs={{0,16},{8,24},{16,0},{24,8},{1,17},{9,25},{17,1},{25,9},{2,18},{10... | collective-permute-start | bytes 98312 | tf_op jit(solution)/shard_map/while/body/eval_jaxpr/ppermute | solution.py:25
  119.1 5.4 %collective-permute-start.5 = (f32[8192]{0:T(1024)S(1)}, f32[8192]{0:T(1024)S(1)}, u32[]{:S(2)}, u32[]{:S(2)}) collective-permute-start(f32[8192]{0:T(1024)S(1)} %add_add_fusion.4), channel_id=1, source_target_pairs={{0,64},{32,96},{64,0},{96,32},{1,65},{33,97},{65,1},{97,33},{2,66}... | collective-permute-start | bytes 98312 | tf_op jit(solution)/shard_map/while/body/eval_jaxpr/ppermute | solution.py:25
  120.3 5.1 %collective-permute-start.6 = (f32[8192]{0:T(1024)S(1)}, f32[8192]{0:T(1024)S(1)}, u32[]{:S(2)}, u32[]{:S(2)}) collective-permute-start(f32[8192]{0:T(1024)S(1)} %add_add_fusion.4), channel_id=1, source_target_pairs={{0,32},{32,64},{64,96},{96,0},{1,33},{33,65},{65,97},{97,1},{2,34}... | collective-permute-start | bytes 98312 | tf_op jit(solution)/shard_map/while/body/eval_jaxpr/ppermute | solution.py:25
  128.4 5.2 %collective-permute-start.8 = (f32[512]{0:T(512)S(1)}, f32[512]{0:T(512)S(1)}, u32[]{:S(2)}, u32[]{:S(2)}) collective-permute-start(f32[512]{0:T(512)S(1)} %bitcast.170), channel_id=1, source_target_pairs={{0,2},{1,3},{2,0},{3,1},{4,6},{5,7},{6,4},{7,5},{8,10},{9,11},{10,... | collective-permute-start | bytes 6152 | tf_op jit(solution)/shard_map/while/body/eval_jaxpr/ppermute | solution.py:25
  129.4 5.3 %collective-permute-start.9 = (f32[512]{0:T(512)S(1)}, f32[512]{0:T(512)S(1)}, u32[]{:S(2)}, u32[]{:S(2)}) collective-permute-start(f32[512]{0:T(512)S(1)} %bitcast.171), channel_id=1, source_target_pairs={{0,1},{1,2},{2,3},{3,0},{4,5},{5,6},{6,7},{7,4},{8,9},{9,10},{10,1... | collective-permute-start | bytes 6152 | tf_op jit(solution)/shard_map/while/body/eval_jaxpr/ppermute | solution.py:25
  148.2 8.2 %collective-permute-start.40 = (bf16[512,256]{1,0:T(8,128)(2,1)S(1)}, bf16[512,256]{1,0:T(8,128)(2,1)S(1)}, u32[]{:S(2)}, u32[]{:S(2)}) collective-permute-start(bf16[512,256]{1,0:T(8,128)(2,1)S(1)} %get-tuple-element.78), channel_id=1, source_target_pairs={{0,1},{1,2},{2,3},{3,0},{4,5},{5,6},{6,7},{7,4},{8,9},{9,10},{10,1... | collective-permute-start | bytes 786440 | tf_op jit(solution)/shard_map/ppermute | solution.py:25
  149.2 10.1 %collective-permute-start.41 = (bf16[512,256]{1,0:T(8,128)(2,1)S(1)}, bf16[512,256]{1,0:T(8,128)(2,1)S(1)}, u32[]{:S(2)}, u32[]{:S(2)}) collective-permute-start(bf16[512,256]{1,0:T(8,128)(2,1)S(1)} %get-tuple-element.78), channel_id=1, source_target_pairs={{0,2},{1,3},{2,0},{3,1},{4,6},{5,7},{6,4},{7,5},{8,10},{9,11},{10,... | collective-permute-start | bytes 786440 | tf_op jit(solution)/shard_map/ppermute | solution.py:25
  151.8 8.1 %collective-permute-start.42 = (bf16[512,256]{1,0:T(8,128)(2,1)S(1)}, bf16[512,256]{1,0:T(8,128)(2,1)S(1)}, u32[]{:S(2)}, u32[]{:S(2)}) collective-permute-start(bf16[512,256]{1,0:T(8,128)(2,1)S(1)} %get-tuple-element.78), channel_id=1, source_target_pairs={{0,3},{1,0},{2,1},{3,2},{4,7},{5,4},{6,5},{7,6},{8,11},{9,8},{10,9... | collective-permute-start | bytes 786440 | tf_op jit(solution)/shard_map/ppermute | solution.py:25
  161.1 16.3 %collective-permute-start.26 = (bf16[4,4,8,4096]{3,2,1,0:T(8,128)(2,1)S(1)}, bf16[4,4,8,4096]{3,2,1,0:T(8,128)(2,1)S(1)}, u32[]{:S(2)}, u32[]{:S(2)}) collective-permute-start(bf16[4,4,8,4096]{3,2,1,0:T(8,128)(2,1)S(1)} %fusion.13), channel_id=1, source_target_pairs={{0,4},{4,0},{1,5},{5,1},{2,6},{6,2},{3,7},{7,3},{8,12},{12,8},{9,1... | collective-permute-start | bytes 3145736 | tf_op jit(solution)/shard_map/ppermute | solution.py:25
  162.3 4.6 %collective-permute-start.44 = (bf16[4,8,512]{2,1,0:T(8,128)(2,1)S(1)}, bf16[4,8,512]{2,1,0:T(8,128)(2,1)S(1)}, u32[]{:S(2)}, u32[]{:S(2)}) collective-permute-start(bf16[4,8,512]{2,1,0:T(8,128)(2,1)S(1)} %get-tuple-element.70), channel_id=1, source_target_pairs={{0,8},{8,16},{16,24},{24,0},{1,9},{9,17},{17,25},{25,1},{2,10},{10... | collective-permute-start | bytes 98312 | tf_op jit(solution)/shard_map/ppermute | solution.py:25
  164.7 5.4 %collective-permute-start.45 = (bf16[4,8,512]{2,1,0:T(8,128)(2,1)S(1)}, bf16[4,8,512]{2,1,0:T(8,128)(2,1)S(1)}, u32[]{:S(2)}, u32[]{:S(2)}) collective-permute-start(bf16[4,8,512]{2,1,0:T(8,128)(2,1)S(1)} %get-tuple-element.72), channel_id=1, source_target_pairs={{0,16},{8,24},{16,0},{24,8},{1,17},{9,25},{17,1},{25,9},{2,18},{10... | collective-permute-start | bytes 98312 | tf_op jit(solution)/shard_map/ppermute | solution.py:25
  164.7 5.5 %collective-permute-start.46 = (bf16[4,8,512]{2,1,0:T(8,128)(2,1)S(1)}, bf16[4,8,512]{2,1,0:T(8,128)(2,1)S(1)}, u32[]{:S(2)}, u32[]{:S(2)}) collective-permute-start(bf16[4,8,512]{2,1,0:T(8,128)(2,1)S(1)} %get-tuple-element.71), channel_id=1, source_target_pairs={{0,24},{8,0},{16,8},{24,16},{1,25},{9,1},{17,9},{25,17},{2,26},{10... | collective-permute-start | bytes 98312 | tf_op jit(solution)/shard_map/ppermute | solution.py:25
  170.2 4.9 %collective-permute-start.47 = (bf16[8,512]{1,0:T(8,128)(2,1)S(1)}, bf16[8,512]{1,0:T(8,128)(2,1)S(1)}, u32[]{:S(2)}, u32[]{:S(2)}) collective-permute-start(bf16[8,512]{1,0:T(8,128)(2,1)S(1)} %get-tuple-element.73), channel_id=1, source_target_pairs={{0,32},{32,64},{64,96},{96,0},{1,33},{33,65},{65,97},{97,1},{2,34}... | collective-permute-start | bytes 24584 | tf_op jit(solution)/shard_map/ppermute | solution.py:25
  170.7 5.2 %collective-permute-start.48 = (bf16[8,512]{1,0:T(8,128)(2,1)S(1)}, bf16[8,512]{1,0:T(8,128)(2,1)S(1)}, u32[]{:S(2)}, u32[]{:S(2)}) collective-permute-start(bf16[8,512]{1,0:T(8,128)(2,1)S(1)} %get-tuple-element.75), channel_id=1, source_target_pairs={{0,64},{32,96},{64,0},{96,32},{1,65},{33,97},{65,1},{97,33},{2,66}... | collective-permute-start | bytes 24584 | tf_op jit(solution)/shard_map/ppermute | solution.py:25
  174.2 7.0 %collective-permute-start.33 = (bf16[4,4,8,4096]{3,2,0,1:T(8,128)(2,1)S(1)}, bf16[4,4,8,4096]{3,2,0,1:T(8,128)(2,1)S(1)}, u32[]{:S(2)}, u32[]{:S(2)}) collective-permute-start(bf16[4,4,8,4096]{3,2,0,1:T(8,128)(2,1)S(1)} %fusion.14), channel_id=1, source_target_pairs={{0,4},{4,0},{1,5},{5,1},{2,6},{6,2},{3,7},{7,3},{8,12},{12,8},{9,1... | collective-permute-start | bytes 3145736 | tf_op jit(solution)/shard_map/ppermute | solution.py:25
  177.7 10.5 %collective-permute-start.27 = (bf16[4,8,4096]{2,1,0:T(8,128)(2,1)S(1)}, bf16[4,8,4096]{2,1,0:T(8,128)(2,1)S(1)}, u32[]{:S(2)}, u32[]{:S(2)}) collective-permute-start(bf16[4,8,4096]{2,1,0:T(8,128)(2,1)S(1)} %get-tuple-element.55), channel_id=1, source_target_pairs={{0,8},{8,16},{16,24},{24,0},{1,9},{9,17},{17,25},{25,1},{2,10},{10... | collective-permute-start | bytes 786440 | tf_op jit(solution)/shard_map/ppermute | solution.py:25
  178.7 10.7 %collective-permute-start.28 = (bf16[4,8,4096]{2,1,0:T(8,128)(2,1)S(1)}, bf16[4,8,4096]{2,1,0:T(8,128)(2,1)S(1)}, u32[]{:S(2)}, u32[]{:S(2)}) collective-permute-start(bf16[4,8,4096]{2,1,0:T(8,128)(2,1)S(1)} %get-tuple-element.57), channel_id=1, source_target_pairs={{0,16},{8,24},{16,0},{24,8},{1,17},{9,25},{17,1},{25,9},{2,18},{10... | collective-permute-start | bytes 786440 | tf_op jit(solution)/shard_map/ppermute | solution.py:25
  179.9 16.0 %collective-permute-start.29 = (bf16[4,8,4096]{2,1,0:T(8,128)(2,1)S(1)}, bf16[4,8,4096]{2,1,0:T(8,128)(2,1)S(1)}, u32[]{:S(2)}, u32[]{:S(2)}) collective-permute-start(bf16[4,8,4096]{2,1,0:T(8,128)(2,1)S(1)} %get-tuple-element.56), channel_id=1, source_target_pairs={{0,24},{8,0},{16,8},{24,16},{1,25},{9,1},{17,9},{25,17},{2,26},{10... | collective-permute-start | bytes 786440 | tf_op jit(solution)/shard_map/ppermute | solution.py:25
  181.6 18.2 %collective-permute-start.34 = (bf16[4,8,4096]{2,1,0:T(8,128)(2,1)S(1)}, bf16[4,8,4096]{2,1,0:T(8,128)(2,1)S(1)}, u32[]{:S(2)}, u32[]{:S(2)}) collective-permute-start(bf16[4,8,4096]{2,1,0:T(8,128)(2,1)S(1)} %get-tuple-element.58), channel_id=1, source_target_pairs={{0,8},{8,16},{16,24},{24,0},{1,9},{9,17},{17,25},{25,1},{2,10},{10... | collective-permute-start | bytes 786440 | tf_op jit(solution)/shard_map/ppermute | solution.py:25
  183.6 16.8 %collective-permute-start.35 = (bf16[4,8,4096]{2,1,0:T(8,128)(2,1)S(1)}, bf16[4,8,4096]{2,1,0:T(8,128)(2,1)S(1)}, u32[]{:S(2)}, u32[]{:S(2)}) collective-permute-start(bf16[4,8,4096]{2,1,0:T(8,128)(2,1)S(1)} %get-tuple-element.60), channel_id=1, source_target_pairs={{0,16},{8,24},{16,0},{24,8},{1,17},{9,25},{17,1},{25,9},{2,18},{10... | collective-permute-start | bytes 786440 | tf_op jit(solution)/shard_map/ppermute | solution.py:25
  188.3 14.8 %collective-permute-start.36 = (bf16[4,8,4096]{2,1,0:T(8,128)(2,1)S(1)}, bf16[4,8,4096]{2,1,0:T(8,128)(2,1)S(1)}, u32[]{:S(2)}, u32[]{:S(2)}) collective-permute-start(bf16[4,8,4096]{2,1,0:T(8,128)(2,1)S(1)} %get-tuple-element.59), channel_id=1, source_target_pairs={{0,24},{8,0},{16,8},{24,16},{1,25},{9,1},{17,9},{25,17},{2,26},{10... | collective-permute-start | bytes 786440 | tf_op jit(solution)/shard_map/ppermute | solution.py:25
  196.0 10.2 %collective-permute-start.30 = (bf16[8,4096]{1,0:T(8,128)(2,1)S(1)}, bf16[8,4096]{1,0:T(8,128)(2,1)S(1)}, u32[]{:S(2)}, u32[]{:S(2)}) collective-permute-start(bf16[8,4096]{1,0:T(8,128)(2,1)S(1)} %get-tuple-element.61), channel_id=1, source_target_pairs={{0,32},{32,64},{64,96},{96,0},{1,33},{33,65},{65,97},{97,1},{2,34}... | collective-permute-start | bytes 196616 | tf_op jit(solution)/shard_map/ppermute | solution.py:25
  197.3 10.9 %collective-permute-start.31 = (bf16[8,4096]{1,0:T(8,128)(2,1)S(1)}, bf16[8,4096]{1,0:T(8,128)(2,1)S(1)}, u32[]{:S(2)}, u32[]{:S(2)}) collective-permute-start(bf16[8,4096]{1,0:T(8,128)(2,1)S(1)} %get-tuple-element.63), channel_id=1, source_target_pairs={{0,64},{32,96},{64,0},{96,32},{1,65},{33,97},{65,1},{97,33},{2,66}... | collective-permute-start | bytes 196616 | tf_op jit(solution)/shard_map/ppermute | solution.py:25
  199.8 8.5 %collective-permute-start.32 = (bf16[8,4096]{1,0:T(8,128)(2,1)S(1)}, bf16[8,4096]{1,0:T(8,128)(2,1)S(1)}, u32[]{:S(2)}, u32[]{:S(2)}) collective-permute-start(bf16[8,4096]{1,0:T(8,128)(2,1)S(1)} %get-tuple-element.62), channel_id=1, source_target_pairs={{0,96},{32,0},{64,32},{96,64},{1,97},{33,1},{65,33},{97,65},{2,98}... | collective-permute-start | bytes 196616 | tf_op jit(solution)/shard_map/ppermute | solution.py:25
  203.2 5.7 %collective-permute-start.37 = (bf16[8,4096]{1,0:T(8,128)(2,1)S(1)}, bf16[8,4096]{1,0:T(8,128)(2,1)S(1)}, u32[]{:S(2)}, u32[]{:S(2)}) collective-permute-start(bf16[8,4096]{1,0:T(8,128)(2,1)S(1)} %get-tuple-element.64), channel_id=1, source_target_pairs={{0,32},{32,64},{64,96},{96,0},{1,33},{33,65},{65,97},{97,1},{2,34}... | collective-permute-start | bytes 196616 | tf_op jit(solution)/shard_map/ppermute | solution.py:25
  204.3 5.8 %collective-permute-start.38 = (bf16[8,4096]{1,0:T(8,128)(2,1)S(1)}, bf16[8,4096]{1,0:T(8,128)(2,1)S(1)}, u32[]{:S(2)}, u32[]{:S(2)}) collective-permute-start(bf16[8,4096]{1,0:T(8,128)(2,1)S(1)} %get-tuple-element.66), channel_id=1, source_target_pairs={{0,64},{32,96},{64,0},{96,32},{1,65},{33,97},{65,1},{97,33},{2,66}... | collective-permute-start | bytes 196616 | tf_op jit(solution)/shard_map/ppermute | solution.py:25
  206.2 4.3 %collective-permute-start.39 = (bf16[8,4096]{1,0:T(8,128)(2,1)S(1)}, bf16[8,4096]{1,0:T(8,128)(2,1)S(1)}, u32[]{:S(2)}, u32[]{:S(2)}) collective-permute-start(bf16[8,4096]{1,0:T(8,128)(2,1)S(1)} %get-tuple-element.65), channel_id=1, source_target_pairs={{0,96},{32,0},{64,32},{96,64},{1,97},{33,1},{65,33},{97,65},{2,98}... | collective-permute-start | bytes 196616 | tf_op jit(solution)/shard_map/ppermute | solution.py:25
  (18 other events, 144.7 us)
where the time goes:
time: 212 us; the launch traced here: 211 us
  starting transfers between devices  72.7 us (34%)
  waiting for transfers between devices  70 us (33%)
  matrix products  26.6 us (13%)
  other arithmetic  24.6 us (12%)
  Pallas kernels  13.6 us (6%)
  local copies, waits for them, and re-layouts  2.47 us (1%)
    ppermute x60, starting transfers between devices, _shift(): return lax.ppermute(v, ax, [(i, (i + k) % n) for i in range(n)])  72.7 us
    ppermute x60, waiting for transfers between devices, _shift(): return lax.ppermute(v, ax, [(i, (i + k) % n) for i in range(n)])  70 us
    pallas_call x1, Pallas kernels, _scores(): pl.pallas_call(_score_kernel, grid=(Pn // bp,), in_specs=[pl.BlockSpec((T...  13.6 us
    convert_element_type x1, other arithmetic, on_device(): dscore = ((probs - plan) * factor).astype(BF16)  11.2 us
    dot_general x3, matrix products, _rowpass(): out = jnp.dot(kern_b, _split(c).T, preferred_element_type=F32)  10.2 us
    dot_general x2, matrix products, _colpass(): out = jnp.dot(_split(r), kern_b, preferred_element_type=F32)  9.45 us
  transfers between devices with their start and end apart: 60, of which 45 were waited for; matrix products, arithmetic and copies ran while one was open for 6% of the time, Pallas kernels for 0%

commit v1 on v0

--- a/solution.py
+++ b/solution.py
@@ -156,19 +156,16 @@
     factor = PROTOS / (soft_temp * math.sqrt(tokens_all))
     dscore = ((probs - plan) * factor).astype(BF16)
     half = dscore.shape[1] // 2
-    pg = []
-    for h in range(2):
-        pg_part = lax.dot_general(
-            unit_b, dscore[:, h * half:(h + 1) * half], (((0,), (0,)), ((), ())), preferred_element_type=F32
-        )
-        pg.append(_rs_dp(pg_part, BF16))
-    proto_grad = jnp.concatenate(pg, axis=1)
+    pg0 = lax.dot_general(unit_b, dscore[:, :half], (((0,), (0,)), ((), ())), preferred_element_type=F32)
+    rs0 = _rs_dp(pg0, BF16)
+    pg1 = lax.dot_general(unit_b, dscore[:, half:], (((0,), (0,)), ((), ())), preferred_element_type=F32)
     dunit_part = lax.dot_general(dscore, normed, (((1,), (1,)), ((), ())), preferred_element_type=F32)
     dunit = _allsum(dunit_part, "z", BF16)
     dproj = ((dunit - unit * jnp.sum(unit * dunit, axis=1, keepdims=True)) / length).astype(BF16)
     head_part = lax.dot_general(dproj, features, (((0,), (0,)), ((), ())), preferred_element_type=F32)
-    head_grad = _rs_dp(head_part, BF16)
-    return (codes, proto_grad, head_grad)
+    rs1 = _rs_dp(jnp.concatenate([pg1, head_part], axis=1), BF16)
+    proto_grad = jnp.concatenate([rs0, rs1[:, :half]], axis=1)
+    return (codes, proto_grad, rs1[:, half:])
 
 
 def solution(mesh):

time: 212 us -> 205 us (0.967)
  starting transfers between devices: 72.7 us -> 61.6 us
  other arithmetic: 24.6 us -> 27.4 us
    ppermute x60 -> x53, starting transfers between devices: 72.7 us -> 61.6 us  [_shift(): return lax.ppermute(v, ax, [(i, (i + k) % n) for i in range(n)])]
    add x10 -> x7, other arithmetic: 1.51 us -> 3.91 us  [_rs(): acc = acc + _shift(blk, ax, k).astype(a.dtype)]
    ppermute x60 -> x53, waiting for transfers between devices: 70 us -> 68.9 us  [_shift(): return lax.ppermute(v, ax, [(i, (i + k) % n) for i in range(n)])]
  transfers between devices with their start and end apart: 60 -> 53, of which waited for: 45 -> 41; matrix products, arithmetic and copies ran while one was open for 6% -> 7% of each run, Pallas kernels for 0% -> 0%
where the time goes in v1:
time: 205 us; the launch traced here: 203 us
  waiting for transfers between devices  68.9 us (34%)
  starting transfers between devices  61.6 us (30%)
  other arithmetic  27.4 us (13%)
  matrix products  26.6 us (13%)
  Pallas kernels  13.5 us (7%)
  local copies, waits for them, and re-layouts  4.04 us (2%)
    ppermute x53, waiting for transfers between devices, _shift(): return lax.ppermute(v, ax, [(i, (i + k) % n) for i in range(n)])  68.9 us
    ppermute x53, starting transfers between devices, _shift(): return lax.ppermute(v, ax, [(i, (i + k) % n) for i in range(n)])  61.6 us
    pallas_call x1, Pallas kernels, _scores(): pl.pallas_call(_score_kernel, grid=(Pn // bp,), in_specs=[pl.BlockSpec((T...  13.5 us
    convert_element_type x1, other arithmetic, on_device(): dscore = ((probs - plan) * factor).astype(BF16)  11.2 us
    dot_general x3, matrix products, _rowpass(): out = jnp.dot(kern_b, _split(c).T, preferred_element_type=F32)  10.2 us
    dot_general x2, matrix products, _colpass(): out = jnp.dot(_split(r), kern_b, preferred_element_type=F32)  9.45 us
  transfers between devices with their start and end apart: 53, of which 41 were waited for; matrix products, arithmetic and copies ran while one was open for 7% of the time, Pallas kernels for 0%

profile of v1, /device:TPU:6, one launch (start us, length us, event | category | flops | bytes accessed | tf_op | source)
XLA Modules:
  0.0 203.2 jit_solution(14920226106347043896)
XLA Ops:
  3.1 2.0 collective-permute-start.10
  5.1 3.6 %collective-permute-start.11 = (f32[128,256]{1,0:T(8,128)S(1)}, f32[128,256]{1,0:T(8,128)S(1)}, u32[]{:S(2)}, u32[]{:S(2)}) collective-permute-start(f32[128,256]{1,0:T(8,128)S(1)} %get-tuple-element.69), channel_id=1, source_target_pairs={{0,2},{1,3},{2,0},{3,1},{4,6},{5,7},{6,4},{7,5},{8,10},{9,11},{10,... | collective-permute-start | bytes 393224 | tf_op jit(solution)/shard_map/ppermute | solution.py:25
  9.7 3.1 %fusion.9 = f32[8192]{0:T(1024)S(1)} fusion(bf16[256,8192]{1,0:T(8,128)(2,1)} %param.7), kind=kLoop, calls=%fused_computation.23 | loop fusion | flops 6283264 | bytes 4227072 | tf_op jit(solution)/shard_map/reduce_sum | solution.py:137
  12.8 2.9 %fusion.10.n_ref = bf16[256,8192]{1,0:T(8,128)(2,1)} fusion(bf16[256,8192]{1,0:T(8,128)(2,1)S(1)} %copy-done.2, f32[8192]{0:T(1024)S(1)} %add_sqrt_fusion), kind=kLoop, calls=%fused_computation.24 | loop fusion | flops 6291456 | bytes 8421376 | tf_op jit(solution)/shard_map/convert_element_type | solution.py:137
  17.1 2.5 %collective-permute-start.15 = (f32[128,256]{1,0:T(8,128)S(1)}, f32[128,256]{1,0:T(8,128)S(1)}, u32[]{:S(2)}, u32[]{:S(2)}) collective-permute-start(f32[128,256]{1,0:T(8,128)S(1)} %fusion.34), channel_id=1, source_target_pairs={{0,3},{1,0},{2,1},{3,2},{4,7},{5,4},{6,5},{7,6},{8,11},{9,8},{10,9... | collective-permute-start | bytes 393224 | tf_op jit(solution)/shard_map/ppermute | solution.py:25
  19.6 3.8 %collective-permute-done.14 = f32[128,256]{1,0:T(8,128)S(1)} collective-permute-done((f32[128,256]{1,0:T(8,128)S(1)}, f32[128,256]{1,0:T(8,128)S(1)}, u32[]{:S(2)}, u32[]{:S(2)}) %collective-permute-start.14) | collective-permute-done | bytes 131104 | tf_op jit(solution)/shard_map/ppermute | solution.py:25
  23.5 2.2 %collective-permute-done.13 = f32[128,256]{1,0:T(8,128)S(1)} collective-permute-done((f32[128,256]{1,0:T(8,128)S(1)}, f32[128,256]{1,0:T(8,128)S(1)}, u32[]{:S(2)}, u32[]{:S(2)}) %collective-permute-start.13) | collective-permute-done | bytes 131104 | tf_op jit(solution)/shard_map/ppermute | solution.py:25
  27.4 13.5 %shard_map.58 = (f32[512,8192]{1,0:T(8,128)}, bf16[512,8192]{1,0:T(8,128)(2,1)}, f32[1,8192]{1,0:T(1,128)}, f32[512,1]{1,0:T(8,128)}) custom-call(bf16[512,256]{1,0:T(8,128)(2,1)} %get-tuple-element.51.u_ref, bf16[256,8192]{1,0:T(8,128)(2,1)} %fusion.10.n_ref), custom_call_target="tpu_custom_call" | custom-call | tf_op jit(solution)/shard_map/pallas_call | solution.py:91
  41.0 1.4 collective-permute-done.16
  43.7 2.4 %collective-permute-start.18 = (f32[8192]{0:T(1024)S(1)}, f32[8192]{0:T(1024)S(1)}, u32[]{:S(2)}, u32[]{:S(2)}) collective-permute-start(f32[8192]{0:T(1024)S(1)} %add.347), channel_id=1, source_target_pairs={{0,16},{8,24},{16,0},{24,8},{1,17},{9,25},{17,1},{25,9},{2,18},{10... | collective-permute-start | bytes 98312 | tf_op jit(solution)/shard_map/ppermute | solution.py:25
  47.2 1.9 collective-permute-done.18
  49.1 2.1 %collective-permute-done.19 = f32[8192]{0:T(1024)S(1)} collective-permute-done((f32[8192]{0:T(1024)S(1)}, f32[8192]{0:T(1024)S(1)}, u32[]{:S(2)}, u32[]{:S(2)}) %collective-permute-start.19) | collective-permute-done | bytes 32800 | tf_op jit(solution)/shard_map/ppermute | solution.py:25
  51.2 1.6 collective-permute-start.20
  52.9 2.9 %collective-permute-start.21 = (f32[8192]{0:T(1024)S(1)}, f32[8192]{0:T(1024)S(1)}, u32[]{:S(2)}, u32[]{:S(2)}) collective-permute-start(f32[8192]{0:T(1024)S(1)} %add_add_fusion.1), channel_id=1, source_target_pairs={{0,64},{32,96},{64,0},{96,32},{1,65},{33,97},{65,1},{97,33},{2,66}... | collective-permute-start | bytes 98312 | tf_op jit(solution)/shard_map/ppermute | solution.py:25
  60.4 5.6 %fusion.41 = f32[512,2]{0,1:T(2,128)S(1)} fusion(bf16[512,8192]{1,0:T(8,128)(2,1)} %get-tuple-element.110, bf16[1,8192]{1,0:T(2,128)(2,1)S(1)} %stack.52, bf16[1,8192]{1,0:T(2,128)(2,1)S(1)} %stack.51), kind=kOutput, calls=%fused_computation.88 | convolution fusion | flops 16842752 | bytes 8425472 | tf_op jit(solution)/shard_map/dot_general | solution.py:123
  66.1 2.0 collective-permute-start.24
  69.5 1.4 collective-permute-done.23
  71.9 62.8 %while.12 = (s32[]{:T(128)}, f32[8192]{0:T(1024)}, f32[512]{0:T(512)S(1)}, bf16[512,8192]{1,0:T(8,128)(2,1)}, s32[]{:T(128)}) while((s32[]{:T(128)}, f32[8192]{0:T(1024)}, f32[512]{0:T(512)S(1)}, bf16[512,8192]{1,0:T(8,128)(2,1)}, s32[]{:T(128)}) %tuple.48), condition=%wide.region_3.4_spmd, body=%wide.region_2.3_spmd.sunk | while | flops 33735168 | bytes 52025832 | solution.py:151
  71.9 4.7 %fusion.72 = f32[2,8192]{1,0:T(2,128)S(1)} fusion(bf16[512,8192]{1,0:T(8,128)(2,1)} %get-tuple-element.120, bf16[1,512]{1,0:T(2,128)(2,1)S(1)} %stack.59, bf16[1,512]{1,0:T(2,128)(2,1)S(1)} %stack.60), kind=kOutput, calls=%fused_computation.10.clone.1 | convolution fusion | flops 16781312 | bytes 8456192 | tf_op jit(solution)/shard_map/while/body/eval_jaxpr/dot_general | solution.py:118
  78.0 2.0 %collective-permute-start.2 = (f32[8192]{0:T(1024)S(1)}, f32[8192]{0:T(1024)S(1)}, u32[]{:S(2)}, u32[]{:S(2)}) collective-permute-start(f32[8192]{0:T(1024)S(1)} %add.526), channel_id=1, source_target_pairs={{0,16},{8,24},{16,0},{24,8},{1,17},{9,25},{17,1},{25,9},{2,18},{10... | collective-permute-start | bytes 98312 | tf_op jit(solution)/shard_map/while/body/eval_jaxpr/ppermute | solution.py:25
  81.2 1.9 collective-permute-done.1
  84.3 2.6 %collective-permute-start.4 = (f32[8192]{0:T(1024)S(1)}, f32[8192]{0:T(1024)S(1)}, u32[]{:S(2)}, u32[]{:S(2)}) collective-permute-start(f32[8192]{0:T(1024)S(1)} %add_add_fusion.4), channel_id=1, source_target_pairs={{0,96},{32,0},{64,32},{96,64},{1,97},{33,1},{65,33},{97,65},{2,98}... | collective-permute-start | bytes 98312 | tf_op jit(solution)/shard_map/while/body/eval_jaxpr/ppermute | solution.py:25
  88.6 3.9 %collective-permute-done.5 = f32[8192]{0:T(1024)S(1)} collective-permute-done((f32[8192]{0:T(1024)S(1)}, f32[8192]{0:T(1024)S(1)}, u32[]{:S(2)}, u32[]{:S(2)}) %collective-permute-start.5) | collective-permute-done | bytes 32800 | tf_op jit(solution)/shard_map/while/body/eval_jaxpr/ppermute | solution.py:25
  93.1 2.3 %convolution_bitcast_fusion.2 = f32[512,2]{0,1:T(2,128)S(1)} fusion(bf16[512,8192]{1,0:T(8,128)(2,1)S(1)} %copy-done.1, bf16[1,8192]{1,0:T(2,128)(2,1)S(1)} %stack.61, bf16[1,8192]{1,0:T(2,128)(2,1)S(1)} %stack.62), kind=kOutput, calls=%fused_computation.1.clone.1 | convolution fusion | flops 16842752 | bytes 8425472 | tf_op jit(solution)/shard_map/while/body/eval_jaxpr/dot_general | solution.py:123
  95.4 2.7 %collective-permute-start.7 = (f32[512]{0:T(512)S(1)}, f32[512]{0:T(512)S(1)}, u32[]{:S(2)}, u32[]{:S(2)}) collective-permute-start(f32[512]{0:T(512)S(1)} %bitcast.135), channel_id=1, source_target_pairs={{0,3},{1,0},{2,1},{3,2},{4,7},{5,4},{6,5},{7,6},{8,11},{9,8},{10,9... | collective-permute-start | bytes 6152 | tf_op jit(solution)/shard_map/while/body/eval_jaxpr/ppermute | solution.py:25
  98.0 1.4 collective-permute-start.8
  99.5 3.7 %collective-permute-done.8 = f32[512]{0:T(512)S(1)} collective-permute-done((f32[512]{0:T(512)S(1)}, f32[512]{0:T(512)S(1)}, u32[]{:S(2)}, u32[]{:S(2)}) %collective-permute-start.8) | collective-permute-done | bytes 2080 | tf_op jit(solution)/shard_map/while/body/eval_jaxpr/ppermute | solution.py:25
  104.3 4.7 %fusion.72 = f32[2,8192]{1,0:T(2,128)S(1)} fusion(bf16[512,8192]{1,0:T(8,128)(2,1)} %get-tuple-element.120, bf16[1,512]{1,0:T(2,128)(2,1)S(1)} %stack.59, bf16[1,512]{1,0:T(2,128)(2,1)S(1)} %stack.60), kind=kOutput, calls=%fused_computation.10.clone.1 | convolution fusion | flops 16781312 | bytes 8456192 | tf_op jit(solution)/shard_map/while/body/eval_jaxpr/dot_general | solution.py:118
  110.4 1.7 collective-permute-start.1
  112.1 2.2 %collective-permute-start.2 = (f32[8192]{0:T(1024)S(1)}, f32[8192]{0:T(1024)S(1)}, u32[]{:S(2)}, u32[]{:S(2)}) collective-permute-start(f32[8192]{0:T(1024)S(1)} %add.526), channel_id=1, source_target_pairs={{0,16},{8,24},{16,0},{24,8},{1,17},{9,25},{17,1},{25,9},{2,18},{10... | collective-permute-start | bytes 98312 | tf_op jit(solution)/shard_map/while/body/eval_jaxpr/ppermute | solution.py:25
  115.5 2.0 collective-permute-done.2
  122.1 2.4 %collective-permute-done.5 = f32[8192]{0:T(1024)S(1)} collective-permute-done((f32[8192]{0:T(1024)S(1)}, f32[8192]{0:T(1024)S(1)}, u32[]{:S(2)}, u32[]{:S(2)}) %collective-permute-start.5) | collective-permute-done | bytes 32800 | tf_op jit(solution)/shard_map/while/body/eval_jaxpr/ppermute | solution.py:25
  126.1 2.3 %convolution_bitcast_fusion.2 = f32[512,2]{0,1:T(2,128)S(1)} fusion(bf16[512,8192]{1,0:T(8,128)(2,1)S(1)} %copy-done.1, bf16[1,8192]{1,0:T(2,128)(2,1)S(1)} %stack.61, bf16[1,8192]{1,0:T(2,128)(2,1)S(1)} %stack.62), kind=kOutput, calls=%fused_computation.1.clone.1 | convolution fusion | flops 16842752 | bytes 8425472 | tf_op jit(solution)/shard_map/while/body/eval_jaxpr/dot_general | solution.py:123
  132.0 1.6 collective-permute-done.8
  134.6 11.2 %multiply_convert_fusion = (bf16[512,8192]{1,0:T(8,128)(2,1)S(1)}, bf16[512,8192]{1,0:T(8,128)(2,1)}) fusion(f32[512,8192]{1,0:T(8,128)} %get-tuple-element.29, f32[512]{0:T(512)S(1)} %bitcast.147, f32[512]{0:T(512)S(1)} %get-tuple-element.34, f32[8192]{0:T(1024)} %get-tuple-element.33), kind=kLoop, calls=%fused_computation.18 | loop fusion | flops 37748736 | bytes 33591296 | tf_op jit(solution)/shard_map/convert_element_type | solution.py:157
  145.8 2.4 %fusion.51 = (bf16[512,256]{1,0:T(8,128)(2,1)S(1)}, f32[512,256]{1,0:T(8,128)S(1)}) fusion(bf16[512,8192]{1,0:T(8,128)(2,1)S(1)} %get-tuple-element.53, bf16[256,8192]{1,0:T(8,128)(2,1)S(1)} %copy-done.3), kind=kOutput, calls=%fused_computation.114 | convolution fusion | flops 2147614720 | bytes 13369344 | tf_op jit(solution)/shard_map/dot_general | solution.py:162
  149.1 2.6 %collective-permute-start.34 = (bf16[512,256]{1,0:T(8,128)(2,1)S(1)}, bf16[512,256]{1,0:T(8,128)(2,1)S(1)}, u32[]{:S(2)}, u32[]{:S(2)}) collective-permute-start(bf16[512,256]{1,0:T(8,128)(2,1)S(1)} %get-tuple-element.72), channel_id=1, source_target_pairs={{0,2},{1,3},{2,0},{3,1},{4,6},{5,7},{6,4},{7,5},{8,10},{9,11},{10,... | collective-permute-start | bytes 786440 | tf_op jit(solution)/shard_map/ppermute | solution.py:25
  154.9 1.5 collective-permute-done.33
  156.4 2.8 %collective-permute-done.34 = bf16[512,256]{1,0:T(8,128)(2,1)S(1)} collective-permute-done((bf16[512,256]{1,0:T(8,128)(2,1)S(1)}, bf16[512,256]{1,0:T(8,128)(2,1)S(1)}, u32[]{:S(2)}, u32[]{:S(2)}) %collective-permute-start.34) | collective-permute-done | bytes 262176 | tf_op jit(solution)/shard_map/ppermute | solution.py:25
  161.5 2.3 %collective-permute-start.27 = (bf16[4,8,4096]{2,1,0:T(8,128)(2,1)S(1)}, bf16[4,8,4096]{2,1,0:T(8,128)(2,1)}, u32[]{:S(2)}, u32[]{:S(2)}) collective-permute-start(bf16[4,8,4096]{2,1,0:T(8,128)(2,1)S(1)} %get-tuple-element.58), channel_id=1, source_target_pairs={{0,8},{8,16},{16,24},{24,0},{1,9},{9,17},{17,25},{25,1},{2,10},{10... | collective-permute-start | bytes 786440 | tf_op jit(solution)/shard_map/ppermute | solution.py:25
  165.9 5.9 %collective-permute-done.27 = bf16[4,8,4096]{2,1,0:T(8,128)(2,1)} collective-permute-done((bf16[4,8,4096]{2,1,0:T(8,128)(2,1)S(1)}, bf16[4,8,4096]{2,1,0:T(8,128)(2,1)}, u32[]{:S(2)}, u32[]{:S(2)}) %collective-permute-start.27) | collective-permute-done | bytes 262176 | tf_op jit(solution)/shard_map/ppermute | solution.py:25
  172.9 2.4 %collective-permute-done.29 = bf16[4,8,4096]{2,1,0:T(8,128)(2,1)} collective-permute-done((bf16[4,8,4096]{2,1,0:T(8,128)(2,1)S(1)}, bf16[4,8,4096]{2,1,0:T(8,128)(2,1)}, u32[]{:S(2)}, u32[]{:S(2)}) %collective-permute-start.29) | collective-permute-done | bytes 262176 | tf_op jit(solution)/shard_map/ppermute | solution.py:25
  176.5 2.3 %bitcast_add_fusion = f32[4,4,8,4608]{3,2,0,1:T(8,128)S(1)} fusion(bf16[4,4,8,4608]{3,2,0,1:T(8,128)(2,1)} %collective-permute-done.36, f32[4,4,2,8,4608]{4,3,2,1,0:T(8,128)} %bitcast.127, s32[]{:T(128)S(6)} %select_n.148), kind=kLoop, calls=%fused_computation.31 | loop fusion | flops 1179648 | bytes 5898244 | tf_op jit(solution)/shard_map/add | solution.py:50
  181.8 2.1 %collective-permute-start.31 = (bf16[8,4096]{1,0:T(8,128)(2,1)S(1)}, bf16[8,4096]{1,0:T(8,128)(2,1)S(1)}, u32[]{:S(2)}, u32[]{:S(2)}) collective-permute-start(bf16[8,4096]{1,0:T(8,128)(2,1)S(1)} %get-tuple-element.66), channel_id=1, source_target_pairs={{0,64},{32,96},{64,0},{96,32},{1,65},{33,97},{65,1},{97,33},{2,66}... | collective-permute-start | bytes 196616 | tf_op jit(solution)/shard_map/ppermute | solution.py:25
  183.9 4.9 %collective-permute-done.37 = bf16[4,8,4608]{2,1,0:T(8,128)(2,1)S(1)} collective-permute-done((bf16[4,8,4608]{2,1,0:T(8,128)(2,1)S(1)}, bf16[4,8,4608]{2,1,0:T(8,128)(2,1)S(1)}, u32[]{:S(2)}, u32[]{:S(2)}) %collective-permute-start.37) | collective-permute-done | bytes 294944 | tf_op jit(solution)/shard_map/ppermute | solution.py:25
  191.1 3.1 %collective-permute-done.39 = bf16[4,8,4608]{2,1,0:T(8,128)(2,1)S(1)} collective-permute-done((bf16[4,8,4608]{2,1,0:T(8,128)(2,1)S(1)}, bf16[4,8,4608]{2,1,0:T(8,128)(2,1)S(1)}, u32[]{:S(2)}, u32[]{:S(2)}) %collective-permute-start.39) | collective-permute-done | bytes 294944 | tf_op jit(solution)/shard_map/ppermute | solution.py:25
  195.4 1.9 collective-permute-start.41
  198.6 3.0 %collective-permute-done.40 = bf16[8,4608]{1,0:T(8,128)(2,1)S(1)} collective-permute-done((bf16[8,4608]{1,0:T(8,128)(2,1)S(1)}, bf16[8,4608]{1,0:T(8,128)(2,1)S(1)}, u32[]{:S(2)}, u32[]{:S(2)}) %collective-permute-start.40) | collective-permute-done | bytes 73760 | tf_op jit(solution)/shard_map/ppermute | solution.py:25
  (147 shorter events, 56.8 us)
Async XLA Ops:
  3.1 12.6 %collective-permute-start.10 = (f32[128,256]{1,0:T(8,128)S(1)}, f32[128,256]{1,0:T(8,128)S(1)}, u32[]{:S(2)}, u32[]{:S(2)}) collective-permute-start(f32[128,256]{1,0:T(8,128)S(1)} %get-tuple-element.67), channel_id=1, source_target_pairs={{0,1},{1,2},{2,3},{3,0},{4,5},{5,6},{6,7},{7,4},{8,9},{9,10},{10,1... | collective-permute-start | bytes 393224 | tf_op jit(solution)/shard_map/ppermute | solution.py:25
  5.1 10.6 %collective-permute-start.11 = (f32[128,256]{1,0:T(8,128)S(1)}, f32[128,256]{1,0:T(8,128)S(1)}, u32[]{:S(2)}, u32[]{:S(2)}) collective-permute-start(f32[128,256]{1,0:T(8,128)S(1)} %get-tuple-element.69), channel_id=1, source_target_pairs={{0,2},{1,3},{2,0},{3,1},{4,6},{5,7},{6,4},{7,5},{8,10},{9,11},{10,... | collective-permute-start | bytes 393224 | tf_op jit(solution)/shard_map/ppermute | solution.py:25
  8.7 7.0 %collective-permute-start.12 = (f32[128,256]{1,0:T(8,128)S(1)}, f32[128,256]{1,0:T(8,128)S(1)}, u32[]{:S(2)}, u32[]{:S(2)}) collective-permute-start(f32[128,256]{1,0:T(8,128)S(1)} %get-tuple-element.68), channel_id=1, source_target_pairs={{0,3},{1,0},{2,1},{3,2},{4,7},{5,4},{6,5},{7,6},{8,11},{9,8},{10,9... | collective-permute-start | bytes 393224 | tf_op jit(solution)/shard_map/ppermute | solution.py:25
  15.8 7.6 %collective-permute-start.14 = (f32[128,256]{1,0:T(8,128)S(1)}, f32[128,256]{1,0:T(8,128)S(1)}, u32[]{:S(2)}, u32[]{:S(2)}) collective-permute-start(f32[128,256]{1,0:T(8,128)S(1)} %fusion.34), channel_id=1, source_target_pairs={{0,2},{1,3},{2,0},{3,1},{4,6},{5,7},{6,4},{7,5},{8,10},{9,11},{10,... | collective-permute-start | bytes 393224 | tf_op jit(solution)/shard_map/ppermute | solution.py:25
  17.1 6.4 %collective-permute-start.15 = (f32[128,256]{1,0:T(8,128)S(1)}, f32[128,256]{1,0:T(8,128)S(1)}, u32[]{:S(2)}, u32[]{:S(2)}) collective-permute-start(f32[128,256]{1,0:T(8,128)S(1)} %fusion.34), channel_id=1, source_target_pairs={{0,3},{1,0},{2,1},{3,2},{4,7},{5,4},{6,5},{7,6},{8,11},{9,8},{10,9... | collective-permute-start | bytes 393224 | tf_op jit(solution)/shard_map/ppermute | solution.py:25
  19.6 6.2 %collective-permute-start.13 = (f32[128,256]{1,0:T(8,128)S(1)}, f32[128,256]{1,0:T(8,128)S(1)}, u32[]{:S(2)}, u32[]{:S(2)}) collective-permute-start(f32[128,256]{1,0:T(8,128)S(1)} %fusion.34), channel_id=1, source_target_pairs={{0,1},{1,2},{2,3},{3,0},{4,5},{5,6},{6,7},{7,4},{8,9},{9,10},{10,1... | collective-permute-start | bytes 393224 | tf_op jit(solution)/shard_map/ppermute | solution.py:25
  43.2 4.0 %collective-permute-start.17 = (f32[8192]{0:T(1024)S(1)}, f32[8192]{0:T(1024)S(1)}, u32[]{:S(2)}, u32[]{:S(2)}) collective-permute-start(f32[8192]{0:T(1024)S(1)} %add.347), channel_id=1, source_target_pairs={{0,8},{8,16},{16,24},{24,0},{1,9},{9,17},{17,25},{25,1},{2,10},{10... | collective-permute-start | bytes 98312 | tf_op jit(solution)/shard_map/ppermute | solution.py:25
  43.7 5.4 %collective-permute-start.18 = (f32[8192]{0:T(1024)S(1)}, f32[8192]{0:T(1024)S(1)}, u32[]{:S(2)}, u32[]{:S(2)}) collective-permute-start(f32[8192]{0:T(1024)S(1)} %add.347), channel_id=1, source_target_pairs={{0,16},{8,24},{16,0},{24,8},{1,17},{9,25},{17,1},{25,9},{2,18},{10... | collective-permute-start | bytes 98312 | tf_op jit(solution)/shard_map/ppermute | solution.py:25
  46.1 5.1 %collective-permute-start.19 = (f32[8192]{0:T(1024)S(1)}, f32[8192]{0:T(1024)S(1)}, u32[]{:S(2)}, u32[]{:S(2)}) collective-permute-start(f32[8192]{0:T(1024)S(1)} %add.347), channel_id=1, source_target_pairs={{0,24},{8,0},{16,8},{24,16},{1,25},{9,1},{17,9},{25,17},{2,26},{10... | collective-permute-start | bytes 98312 | tf_op jit(solution)/shard_map/ppermute | solution.py:25
  51.2 7.0 %collective-permute-start.20 = (f32[8192]{0:T(1024)S(1)}, f32[8192]{0:T(1024)S(1)}, u32[]{:S(2)}, u32[]{:S(2)}) collective-permute-start(f32[8192]{0:T(1024)S(1)} %add_add_fusion.1), channel_id=1, source_target_pairs={{0,32},{32,64},{64,96},{96,0},{1,33},{33,65},{65,97},{97,1},{2,34}... | collective-permute-start | bytes 98312 | tf_op jit(solution)/shard_map/ppermute | solution.py:25
  52.9 5.4 %collective-permute-start.21 = (f32[8192]{0:T(1024)S(1)}, f32[8192]{0:T(1024)S(1)}, u32[]{:S(2)}, u32[]{:S(2)}) collective-permute-start(f32[8192]{0:T(1024)S(1)} %add_add_fusion.1), channel_id=1, source_target_pairs={{0,64},{32,96},{64,0},{96,32},{1,65},{33,97},{65,1},{97,33},{2,66}... | collective-permute-start | bytes 98312 | tf_op jit(solution)/shard_map/ppermute | solution.py:25
  55.8 3.9 %collective-permute-start.22 = (f32[8192]{0:T(1024)S(1)}, f32[8192]{0:T(1024)S(1)}, u32[]{:S(2)}, u32[]{:S(2)}) collective-permute-start(f32[8192]{0:T(1024)S(1)} %add_add_fusion.1), channel_id=1, source_target_pairs={{0,96},{32,0},{64,32},{96,64},{1,97},{33,1},{65,33},{97,65},{2,98}... | collective-permute-start | bytes 98312 | tf_op jit(solution)/shard_map/ppermute | solution.py:25
  66.0 4.9 %collective-permute-start.23 = (f32[2,512]{1,0:T(2,128)S(1)}, f32[2,512]{1,0:T(2,128)S(1)}, u32[]{:S(2)}, u32[]{:S(2)}) collective-permute-start(f32[2,512]{1,0:T(2,128)S(1)} %pad_maximum_fusion.3), channel_id=1, source_target_pairs={{0,1},{1,2},{2,3},{3,0},{4,5},{5,6},{6,7},{7,4},{8,9},{9,10},{10,1... | collective-permute-start | bytes 12296 | tf_op jit(solution)/shard_map/ppermute | solution.py:25
  66.1 5.2 %collective-permute-start.24 = (f32[2,512]{1,0:T(2,128)S(1)}, f32[2,512]{1,0:T(2,128)S(1)}, u32[]{:S(2)}, u32[]{:S(2)}) collective-permute-start(f32[2,512]{1,0:T(2,128)S(1)} %pad_maximum_fusion.3), channel_id=1, source_target_pairs={{0,2},{1,3},{2,0},{3,1},{4,6},{5,7},{6,4},{7,5},{8,10},{9,11},{10,... | collective-permute-start | bytes 12296 | tf_op jit(solution)/shard_map/ppermute | solution.py:25
  78.0 5.1 %collective-permute-start.1 = (f32[8192]{0:T(1024)S(1)}, f32[8192]{0:T(1024)S(1)}, u32[]{:S(2)}, u32[]{:S(2)}) collective-permute-start(f32[8192]{0:T(1024)S(1)} %add.526), channel_id=1, source_target_pairs={{0,24},{8,0},{16,8},{24,16},{1,25},{9,1},{17,9},{25,17},{2,26},{10... | collective-permute-start | bytes 98312 | tf_op jit(solution)/shard_map/while/body/eval_jaxpr/ppermute | solution.py:25
  78.0 5.5 %collective-permute-start.2 = (f32[8192]{0:T(1024)S(1)}, f32[8192]{0:T(1024)S(1)}, u32[]{:S(2)}, u32[]{:S(2)}) collective-permute-start(f32[8192]{0:T(1024)S(1)} %add.526), channel_id=1, source_target_pairs={{0,16},{8,24},{16,0},{24,8},{1,17},{9,25},{17,1},{25,9},{2,18},{10... | collective-permute-start | bytes 98312 | tf_op jit(solution)/shard_map/while/body/eval_jaxpr/ppermute | solution.py:25
  80.0 4.3 %collective-permute-start.3 = (f32[8192]{0:T(1024)S(1)}, f32[8192]{0:T(1024)S(1)}, u32[]{:S(2)}, u32[]{:S(2)}) collective-permute-start(f32[8192]{0:T(1024)S(1)} %add.526), channel_id=1, source_target_pairs={{0,8},{8,16},{16,24},{24,0},{1,9},{9,17},{17,25},{25,1},{2,10},{10... | collective-permute-start | bytes 98312 | tf_op jit(solution)/shard_map/while/body/eval_jaxpr/ppermute | solution.py:25
  84.3 4.2 %collective-permute-start.4 = (f32[8192]{0:T(1024)S(1)}, f32[8192]{0:T(1024)S(1)}, u32[]{:S(2)}, u32[]{:S(2)}) collective-permute-start(f32[8192]{0:T(1024)S(1)} %add_add_fusion.4), channel_id=1, source_target_pairs={{0,96},{32,0},{64,32},{96,64},{1,97},{33,1},{65,33},{97,65},{2,98}... | collective-permute-start | bytes 98312 | tf_op jit(solution)/shard_map/while/body/eval_jaxpr/ppermute | solution.py:25
  87.0 5.5 %collective-permute-start.5 = (f32[8192]{0:T(1024)S(1)}, f32[8192]{0:T(1024)S(1)}, u32[]{:S(2)}, u32[]{:S(2)}) collective-permute-start(f32[8192]{0:T(1024)S(1)} %add_add_fusion.4), channel_id=1, source_target_pairs={{0,64},{32,96},{64,0},{96,32},{1,65},{33,97},{65,1},{97,33},{2,66}... | collective-permute-start | bytes 98312 | tf_op jit(solution)/shard_map/while/body/eval_jaxpr/ppermute | solution.py:25
  87.0 5.5 %collective-permute-start.6 = (f32[8192]{0:T(1024)S(1)}, f32[8192]{0:T(1024)S(1)}, u32[]{:S(2)}, u32[]{:S(2)}) collective-permute-start(f32[8192]{0:T(1024)S(1)} %add_add_fusion.4), channel_id=1, source_target_pairs={{0,32},{32,64},{64,96},{96,0},{1,33},{33,65},{65,97},{97,1},{2,34}... | collective-permute-start | bytes 98312 | tf_op jit(solution)/shard_map/while/body/eval_jaxpr/ppermute | solution.py:25
  95.4 4.1 %collective-permute-start.7 = (f32[512]{0:T(512)S(1)}, f32[512]{0:T(512)S(1)}, u32[]{:S(2)}, u32[]{:S(2)}) collective-permute-start(f32[512]{0:T(512)S(1)} %bitcast.135), channel_id=1, source_target_pairs={{0,3},{1,0},{2,1},{3,2},{4,7},{5,4},{6,5},{7,6},{8,11},{9,8},{10,9... | collective-permute-start | bytes 6152 | tf_op jit(solution)/shard_map/while/body/eval_jaxpr/ppermute | solution.py:25
  98.0 5.1 %collective-permute-start.8 = (f32[512]{0:T(512)S(1)}, f32[512]{0:T(512)S(1)}, u32[]{:S(2)}, u32[]{:S(2)}) collective-permute-start(f32[512]{0:T(512)S(1)} %bitcast.136), channel_id=1, source_target_pairs={{0,2},{1,3},{2,0},{3,1},{4,6},{5,7},{6,4},{7,5},{8,10},{9,11},{10,... | collective-permute-start | bytes 6152 | tf_op jit(solution)/shard_map/while/body/eval_jaxpr/ppermute | solution.py:25
  99.5 4.8 %collective-permute-start.9 = (f32[512]{0:T(512)S(1)}, f32[512]{0:T(512)S(1)}, u32[]{:S(2)}, u32[]{:S(2)}) collective-permute-start(f32[512]{0:T(512)S(1)} %bitcast.137), channel_id=1, source_target_pairs={{0,1},{1,2},{2,3},{3,0},{4,5},{5,6},{6,7},{7,4},{8,9},{9,10},{10,1... | collective-permute-start | bytes 6152 | tf_op jit(solution)/shard_map/while/body/eval_jaxpr/ppermute | solution.py:25
  110.4 5.1 %collective-permute-start.1 = (f32[8192]{0:T(1024)S(1)}, f32[8192]{0:T(1024)S(1)}, u32[]{:S(2)}, u32[]{:S(2)}) collective-permute-start(f32[8192]{0:T(1024)S(1)} %add.526), channel_id=1, source_target_pairs={{0,24},{8,0},{16,8},{24,16},{1,25},{9,1},{17,9},{25,17},{2,26},{10... | collective-permute-start | bytes 98312 | tf_op jit(solution)/shard_map/while/body/eval_jaxpr/ppermute | solution.py:25
  112.1 5.4 %collective-permute-start.2 = (f32[8192]{0:T(1024)S(1)}, f32[8192]{0:T(1024)S(1)}, u32[]{:S(2)}, u32[]{:S(2)}) collective-permute-start(f32[8192]{0:T(1024)S(1)} %add.526), channel_id=1, source_target_pairs={{0,16},{8,24},{16,0},{24,8},{1,17},{9,25},{17,1},{25,9},{2,18},{10... | collective-permute-start | bytes 98312 | tf_op jit(solution)/shard_map/while/body/eval_jaxpr/ppermute | solution.py:25
  114.2 3.9 %collective-permute-start.3 = (f32[8192]{0:T(1024)S(1)}, f32[8192]{0:T(1024)S(1)}, u32[]{:S(2)}, u32[]{:S(2)}) collective-permute-start(f32[8192]{0:T(1024)S(1)} %add.526), channel_id=1, source_target_pairs={{0,8},{8,16},{16,24},{24,0},{1,9},{9,17},{17,25},{25,1},{2,10},{10... | collective-permute-start | bytes 98312 | tf_op jit(solution)/shard_map/while/body/eval_jaxpr/ppermute | solution.py:25
  118.1 4.0 %collective-permute-start.4 = (f32[8192]{0:T(1024)S(1)}, f32[8192]{0:T(1024)S(1)}, u32[]{:S(2)}, u32[]{:S(2)}) collective-permute-start(f32[8192]{0:T(1024)S(1)} %add_add_fusion.4), channel_id=1, source_target_pairs={{0,96},{32,0},{64,32},{96,64},{1,97},{33,1},{65,33},{97,65},{2,98}... | collective-permute-start | bytes 98312 | tf_op jit(solution)/shard_map/while/body/eval_jaxpr/ppermute | solution.py:25
  119.1 5.4 %collective-permute-start.5 = (f32[8192]{0:T(1024)S(1)}, f32[8192]{0:T(1024)S(1)}, u32[]{:S(2)}, u32[]{:S(2)}) collective-permute-start(f32[8192]{0:T(1024)S(1)} %add_add_fusion.4), channel_id=1, source_target_pairs={{0,64},{32,96},{64,0},{96,32},{1,65},{33,97},{65,1},{97,33},{2,66}... | collective-permute-start | bytes 98312 | tf_op jit(solution)/shard_map/while/body/eval_jaxpr/ppermute | solution.py:25
  120.3 5.1 %collective-permute-start.6 = (f32[8192]{0:T(1024)S(1)}, f32[8192]{0:T(1024)S(1)}, u32[]{:S(2)}, u32[]{:S(2)}) collective-permute-start(f32[8192]{0:T(1024)S(1)} %add_add_fusion.4), channel_id=1, source_target_pairs={{0,32},{32,64},{64,96},{96,0},{1,33},{33,65},{65,97},{97,1},{2,34}... | collective-permute-start | bytes 98312 | tf_op jit(solution)/shard_map/while/body/eval_jaxpr/ppermute | solution.py:25
  128.4 5.2 %collective-permute-start.8 = (f32[512]{0:T(512)S(1)}, f32[512]{0:T(512)S(1)}, u32[]{:S(2)}, u32[]{:S(2)}) collective-permute-start(f32[512]{0:T(512)S(1)} %bitcast.136), channel_id=1, source_target_pairs={{0,2},{1,3},{2,0},{3,1},{4,6},{5,7},{6,4},{7,5},{8,10},{9,11},{10,... | collective-permute-start | bytes 6152 | tf_op jit(solution)/shard_map/while/body/eval_jaxpr/ppermute | solution.py:25
  129.4 5.3 %collective-permute-start.9 = (f32[512]{0:T(512)S(1)}, f32[512]{0:T(512)S(1)}, u32[]{:S(2)}, u32[]{:S(2)}) collective-permute-start(f32[512]{0:T(512)S(1)} %bitcast.137), channel_id=1, source_target_pairs={{0,1},{1,2},{2,3},{3,0},{4,5},{5,6},{6,7},{7,4},{8,9},{9,10},{10,1... | collective-permute-start | bytes 6152 | tf_op jit(solution)/shard_map/while/body/eval_jaxpr/ppermute | solution.py:25
  148.2 8.2 %collective-permute-start.33 = (bf16[512,256]{1,0:T(8,128)(2,1)S(1)}, bf16[512,256]{1,0:T(8,128)(2,1)S(1)}, u32[]{:S(2)}, u32[]{:S(2)}) collective-permute-start(bf16[512,256]{1,0:T(8,128)(2,1)S(1)} %get-tuple-element.72), channel_id=1, source_target_pairs={{0,1},{1,2},{2,3},{3,0},{4,5},{5,6},{6,7},{7,4},{8,9},{9,10},{10,1... | collective-permute-start | bytes 786440 | tf_op jit(solution)/shard_map/ppermute | solution.py:25
  149.1 10.1 %collective-permute-start.34 = (bf16[512,256]{1,0:T(8,128)(2,1)S(1)}, bf16[512,256]{1,0:T(8,128)(2,1)S(1)}, u32[]{:S(2)}, u32[]{:S(2)}) collective-permute-start(bf16[512,256]{1,0:T(8,128)(2,1)S(1)} %get-tuple-element.72), channel_id=1, source_target_pairs={{0,2},{1,3},{2,0},{3,1},{4,6},{5,7},{6,4},{7,5},{8,10},{9,11},{10,... | collective-permute-start | bytes 786440 | tf_op jit(solution)/shard_map/ppermute | solution.py:25
  151.7 8.1 %collective-permute-start.35 = (bf16[512,256]{1,0:T(8,128)(2,1)S(1)}, bf16[512,256]{1,0:T(8,128)(2,1)S(1)}, u32[]{:S(2)}, u32[]{:S(2)}) collective-permute-start(bf16[512,256]{1,0:T(8,128)(2,1)S(1)} %get-tuple-element.72), channel_id=1, source_target_pairs={{0,3},{1,0},{2,1},{3,2},{4,7},{5,4},{6,5},{7,6},{8,11},{9,8},{10,9... | collective-permute-start | bytes 786440 | tf_op jit(solution)/shard_map/ppermute | solution.py:25
  153.5 7.6 %collective-permute-start.26 = (bf16[4,4,8,4096]{3,2,1,0:T(8,128)(2,1)S(1)}, bf16[4,4,8,4096]{3,2,1,0:T(8,128)(2,1)S(1)}, u32[]{:S(2)}, u32[]{:S(2)}) collective-permute-start(bf16[4,4,8,4096]{3,2,1,0:T(8,128)(2,1)S(1)} %fusion.15), channel_id=1, source_target_pairs={{0,4},{4,0},{1,5},{5,1},{2,6},{6,2},{3,7},{7,3},{8,12},{12,8},{9,1... | collective-permute-start | bytes 3145736 | tf_op jit(solution)/shard_map/ppermute | solution.py:25
  161.5 10.3 %collective-permute-start.27 = (bf16[4,8,4096]{2,1,0:T(8,128)(2,1)S(1)}, bf16[4,8,4096]{2,1,0:T(8,128)(2,1)}, u32[]{:S(2)}, u32[]{:S(2)}) collective-permute-start(bf16[4,8,4096]{2,1,0:T(8,128)(2,1)S(1)} %get-tuple-element.58), channel_id=1, source_target_pairs={{0,8},{8,16},{16,24},{24,0},{1,9},{9,17},{17,25},{25,1},{2,10},{10... | collective-permute-start | bytes 786440 | tf_op jit(solution)/shard_map/ppermute | solution.py:25
  163.8 9.1 %collective-permute-start.28 = (bf16[4,8,4096]{2,1,0:T(8,128)(2,1)S(1)}, bf16[4,8,4096]{2,1,0:T(8,128)(2,1)}, u32[]{:S(2)}, u32[]{:S(2)}) collective-permute-start(bf16[4,8,4096]{2,1,0:T(8,128)(2,1)S(1)} %get-tuple-element.60), channel_id=1, source_target_pairs={{0,16},{8,24},{16,0},{24,8},{1,17},{9,25},{17,1},{25,9},{2,18},{10... | collective-permute-start | bytes 786440 | tf_op jit(solution)/shard_map/ppermute | solution.py:25
  163.8 11.5 %collective-permute-start.29 = (bf16[4,8,4096]{2,1,0:T(8,128)(2,1)S(1)}, bf16[4,8,4096]{2,1,0:T(8,128)(2,1)}, u32[]{:S(2)}, u32[]{:S(2)}) collective-permute-start(bf16[4,8,4096]{2,1,0:T(8,128)(2,1)S(1)} %get-tuple-element.59), channel_id=1, source_target_pairs={{0,24},{8,0},{16,8},{24,16},{1,25},{9,1},{17,9},{25,17},{2,26},{10... | collective-permute-start | bytes 786440 | tf_op jit(solution)/shard_map/ppermute | solution.py:25
  165.9 10.6 %collective-permute-start.36 = (bf16[4,4,8,4608]{3,2,0,1:T(8,128)(2,1)}, bf16[4,4,8,4608]{3,2,0,1:T(8,128)(2,1)}, u32[]{:S(2)}, u32[]{:S(2)}) collective-permute-start(bf16[4,4,8,4608]{3,2,0,1:T(8,128)(2,1)} %fusion.14), channel_id=1, source_target_pairs={{0,4},{4,0},{1,5},{5,1},{2,6},{6,2},{3,7},{7,3},{8,12},{12,8},{9,1... | collective-permute-start | bytes 3538952 | tf_op jit(solution)/shard_map/ppermute | solution.py:25
  178.9 9.9 %collective-permute-start.37 = (bf16[4,8,4608]{2,1,0:T(8,128)(2,1)S(1)}, bf16[4,8,4608]{2,1,0:T(8,128)(2,1)S(1)}, u32[]{:S(2)}, u32[]{:S(2)}) collective-permute-start(bf16[4,8,4608]{2,1,0:T(8,128)(2,1)S(1)} %get-tuple-element.55), channel_id=1, source_target_pairs={{0,8},{8,16},{16,24},{24,0},{1,9},{9,17},{17,25},{25,1},{2,10},{10... | collective-permute-start | bytes 884744 | tf_op jit(solution)/shard_map/ppermute | solution.py:25
  179.9 11.3 %collective-permute-start.38 = (bf16[4,8,4608]{2,1,0:T(8,128)(2,1)S(1)}, bf16[4,8,4608]{2,1,0:T(8,128)(2,1)S(1)}, u32[]{:S(2)}, u32[]{:S(2)}) collective-permute-start(bf16[4,8,4608]{2,1,0:T(8,128)(2,1)S(1)} %get-tuple-element.57), channel_id=1, source_target_pairs={{0,16},{8,24},{16,0},{24,8},{1,17},{9,25},{17,1},{25,9},{2,18},{10... | collective-permute-start | bytes 884744 | tf_op jit(solution)/shard_map/ppermute | solution.py:25
  180.1 14.1 %collective-permute-start.39 = (bf16[4,8,4608]{2,1,0:T(8,128)(2,1)S(1)}, bf16[4,8,4608]{2,1,0:T(8,128)(2,1)S(1)}, u32[]{:S(2)}, u32[]{:S(2)}) collective-permute-start(bf16[4,8,4608]{2,1,0:T(8,128)(2,1)S(1)} %get-tuple-element.56), channel_id=1, source_target_pairs={{0,24},{8,0},{16,8},{24,16},{1,25},{9,1},{17,9},{25,17},{2,26},{10... | collective-permute-start | bytes 884744 | tf_op jit(solution)/shard_map/ppermute | solution.py:25
  181.0 16.3 %collective-permute-start.30 = (bf16[8,4096]{1,0:T(8,128)(2,1)S(1)}, bf16[8,4096]{1,0:T(8,128)(2,1)S(1)}, u32[]{:S(2)}, u32[]{:S(2)}) collective-permute-start(bf16[8,4096]{1,0:T(8,128)(2,1)S(1)} %get-tuple-element.64), channel_id=1, source_target_pairs={{0,32},{32,64},{64,96},{96,0},{1,33},{33,65},{65,97},{97,1},{2,34}... | collective-permute-start | bytes 196616 | tf_op jit(solution)/shard_map/ppermute | solution.py:25
  181.8 16.8 %collective-permute-start.31 = (bf16[8,4096]{1,0:T(8,128)(2,1)S(1)}, bf16[8,4096]{1,0:T(8,128)(2,1)S(1)}, u32[]{:S(2)}, u32[]{:S(2)}) collective-permute-start(bf16[8,4096]{1,0:T(8,128)(2,1)S(1)} %get-tuple-element.66), channel_id=1, source_target_pairs={{0,64},{32,96},{64,0},{96,32},{1,65},{33,97},{65,1},{97,33},{2,66}... | collective-permute-start | bytes 196616 | tf_op jit(solution)/shard_map/ppermute | solution.py:25
  188.8 9.7 %collective-permute-start.32 = (bf16[8,4096]{1,0:T(8,128)(2,1)S(1)}, bf16[8,4096]{1,0:T(8,128)(2,1)S(1)}, u32[]{:S(2)}, u32[]{:S(2)}) collective-permute-start(bf16[8,4096]{1,0:T(8,128)(2,1)S(1)} %get-tuple-element.65), channel_id=1, source_target_pairs={{0,96},{32,0},{64,32},{96,64},{1,97},{33,1},{65,33},{97,65},{2,98}... | collective-permute-start | bytes 196616 | tf_op jit(solution)/shard_map/ppermute | solution.py:25
  194.4 7.2 %collective-permute-start.40 = (bf16[8,4608]{1,0:T(8,128)(2,1)S(1)}, bf16[8,4608]{1,0:T(8,128)(2,1)S(1)}, u32[]{:S(2)}, u32[]{:S(2)}) collective-permute-start(bf16[8,4608]{1,0:T(8,128)(2,1)S(1)} %get-tuple-element.61), channel_id=1, source_target_pairs={{0,32},{32,64},{64,96},{96,0},{1,33},{33,65},{65,97},{97,1},{2,34}... | collective-permute-start | bytes 221192 | tf_op jit(solution)/shard_map/ppermute | solution.py:25
  195.4 6.2 %collective-permute-start.41 = (bf16[8,4608]{1,0:T(8,128)(2,1)S(1)}, bf16[8,4608]{1,0:T(8,128)(2,1)S(1)}, u32[]{:S(2)}, u32[]{:S(2)}) collective-permute-start(bf16[8,4608]{1,0:T(8,128)(2,1)S(1)} %get-tuple-element.63), channel_id=1, source_target_pairs={{0,64},{32,96},{64,0},{96,32},{1,65},{33,97},{65,1},{97,33},{2,66}... | collective-permute-start | bytes 221192 | tf_op jit(solution)/shard_map/ppermute | solution.py:25
  197.3 4.5 %collective-permute-start.42 = (bf16[8,4608]{1,0:T(8,128)(2,1)S(1)}, bf16[8,4608]{1,0:T(8,128)(2,1)S(1)}, u32[]{:S(2)}, u32[]{:S(2)}) collective-permute-start(bf16[8,4608]{1,0:T(8,128)(2,1)S(1)} %get-tuple-element.62), channel_id=1, source_target_pairs={{0,96},{32,0},{64,32},{96,64},{1,97},{33,1},{65,33},{97,65},{2,98}... | collective-permute-start | bytes 221192 | tf_op jit(solution)/shard_map/ppermute | solution.py:25
  (12 other events, 109.7 us)

commit v2 on v1

--- a/solution.py
+++ b/solution.py
@@ -155,7 +155,7 @@
     tokens_all = 32 * T
     factor = PROTOS / (soft_temp * math.sqrt(tokens_all))
     dscore = ((probs - plan) * factor).astype(BF16)
-    half = dscore.shape[1] // 2
+    half = dscore.shape[1] * 3 // 4
     pg0 = lax.dot_general(unit_b, dscore[:, :half], (((0,), (0,)), ((), ())), preferred_element_type=F32)
     rs0 = _rs_dp(pg0, BF16)
     pg1 = lax.dot_general(unit_b, dscore[:, half:], (((0,), (0,)), ((), ())), preferred_element_type=F32)
@@ -164,8 +164,9 @@
     dproj = ((dunit - unit * jnp.sum(unit * dunit, axis=1, keepdims=True)) / length).astype(BF16)
     head_part = lax.dot_general(dproj, features, (((0,), (0,)), ((), ())), preferred_element_type=F32)
     rs1 = _rs_dp(jnp.concatenate([pg1, head_part], axis=1), BF16)
-    proto_grad = jnp.concatenate([rs0, rs1[:, :half]], axis=1)
-    return (codes, proto_grad, rs1[:, half:])
+    w1 = dscore.shape[1] - half
+    proto_grad = jnp.concatenate([rs0, rs1[:, :w1]], axis=1)
+    return (codes, proto_grad, rs1[:, w1:])
 
 
 def solution(mesh):

time: 205 us -> 206 us (level)
  starting transfers between devices: 61.6 us -> 64.5 us
  waiting for transfers between devices: 68.9 us -> 66.3 us
    ppermute x53, starting transfers between devices: 61.6 us -> 64.5 us  [_shift(): return lax.ppermute(v, ax, [(i, (i + k) % n) for i in range(n)])]
    ppermute x53, waiting for transfers between devices: 68.9 us -> 66.3 us  [_shift(): return lax.ppermute(v, ax, [(i, (i + k) % n) for i in range(n)])]
  transfers between devices with their start and end apart: 53 -> 53, of which waited for: 41 -> 39; matrix products, arithmetic and copies ran while one was open for 7% -> 8% of each run, Pallas kernels for 0% -> 0%
where the time goes in v2:
time: 206 us; the launch traced here: 205 us
  waiting for transfers between devices  66.3 us (32%)
  starting transfers between devices  64.5 us (31%)
  other arithmetic  27.6 us (13%)
  matrix products  26.6 us (13%)
  Pallas kernels  13.6 us (7%)
  local copies, waits for them, and re-layouts  5.16 us (3%)
    ppermute x53, waiting for transfers between devices, _shift(): return lax.ppermute(v, ax, [(i, (i + k) % n) for i in range(n)])  66.3 us
    ppermute x53, starting transfers between devices, _shift(): return lax.ppermute(v, ax, [(i, (i + k) % n) for i in range(n)])  64.5 us
    pallas_call x1, Pallas kernels, _scores(): pl.pallas_call(_score_kernel, grid=(Pn // bp,), in_specs=[pl.BlockSpec((T...  13.6 us
    convert_element_type x1, other arithmetic, on_device(): dscore = ((probs - plan) * factor).astype(BF16)  11.2 us
    dot_general x3, matrix products, _rowpass(): out = jnp.dot(kern_b, _split(c).T, preferred_element_type=F32)  10.2 us
    dot_general x2, matrix products, _colpass(): out = jnp.dot(_split(r), kern_b, preferred_element_type=F32)  9.45 us
    add x7, other arithmetic, _rs(): acc = acc + _shift(blk, ax, k).astype(a.dtype)  4.33 us
  transfers between devices with their start and end apart: 53, of which 39 were waited for; matrix products, arithmetic and copies ran while one was open for 8% of the time, Pallas kernels for 0%

profile of v2, /device:TPU:6, one launch (start us, length us, event | category | flops | bytes accessed | tf_op | source)
XLA Modules:
  0.0 204.9 jit_solution(5696760501872021253)
XLA Ops:
  3.1 2.0 collective-permute-start.10
  5.1 3.6 %collective-permute-start.11 = (f32[128,256]{1,0:T(8,128)S(1)}, f32[128,256]{1,0:T(8,128)S(1)}, u32[]{:S(2)}, u32[]{:S(2)}) collective-permute-start(f32[128,256]{1,0:T(8,128)S(1)} %get-tuple-element.66), channel_id=1, source_target_pairs={{0,2},{1,3},{2,0},{3,1},{4,6},{5,7},{6,4},{7,5},{8,10},{9,11},{10,... | collective-permute-start | bytes 393224 | tf_op jit(solution)/shard_map/ppermute | solution.py:25
  9.7 3.1 %fusion.9 = f32[8192]{0:T(1024)S(1)} fusion(bf16[256,8192]{1,0:T(8,128)(2,1)} %param.7), kind=kLoop, calls=%fused_computation.23 | loop fusion | flops 6283264 | bytes 4227072 | tf_op jit(solution)/shard_map/reduce_sum | solution.py:137
  12.8 2.9 %fusion.10.n_ref = bf16[256,8192]{1,0:T(8,128)(2,1)} fusion(bf16[256,8192]{1,0:T(8,128)(2,1)S(1)} %copy-done.3, f32[8192]{0:T(1024)S(1)} %add_sqrt_fusion), kind=kLoop, calls=%fused_computation.24 | loop fusion | flops 6291456 | bytes 8421376 | tf_op jit(solution)/shard_map/convert_element_type | solution.py:137
  17.1 2.5 %collective-permute-start.15 = (f32[128,256]{1,0:T(8,128)S(1)}, f32[128,256]{1,0:T(8,128)S(1)}, u32[]{:S(2)}, u32[]{:S(2)}) collective-permute-start(f32[128,256]{1,0:T(8,128)S(1)} %fusion.32), channel_id=1, source_target_pairs={{0,3},{1,0},{2,1},{3,2},{4,7},{5,4},{6,5},{7,6},{8,11},{9,8},{10,9... | collective-permute-start | bytes 393224 | tf_op jit(solution)/shard_map/ppermute | solution.py:25
  19.6 3.8 %collective-permute-done.14 = f32[128,256]{1,0:T(8,128)S(1)} collective-permute-done((f32[128,256]{1,0:T(8,128)S(1)}, f32[128,256]{1,0:T(8,128)S(1)}, u32[]{:S(2)}, u32[]{:S(2)}) %collective-permute-start.14) | collective-permute-done | bytes 131104 | tf_op jit(solution)/shard_map/ppermute | solution.py:25
  23.5 2.2 %collective-permute-done.13 = f32[128,256]{1,0:T(8,128)S(1)} collective-permute-done((f32[128,256]{1,0:T(8,128)S(1)}, f32[128,256]{1,0:T(8,128)S(1)}, u32[]{:S(2)}, u32[]{:S(2)}) %collective-permute-start.13) | collective-permute-done | bytes 131104 | tf_op jit(solution)/shard_map/ppermute | solution.py:25
  27.4 13.6 %shard_map.58 = (f32[512,8192]{1,0:T(8,128)}, bf16[512,8192]{1,0:T(8,128)(2,1)}, f32[1,8192]{1,0:T(1,128)}, f32[512,1]{1,0:T(8,128)}) custom-call(bf16[512,256]{1,0:T(8,128)(2,1)} %get-tuple-element.51.u_ref, bf16[256,8192]{1,0:T(8,128)(2,1)} %fusion.10.n_ref), custom_call_target="tpu_custom_call" | custom-call | tf_op jit(solution)/shard_map/pallas_call | solution.py:91
  43.7 2.4 %collective-permute-start.18 = (f32[8192]{0:T(1024)S(1)}, f32[8192]{0:T(1024)S(1)}, u32[]{:S(2)}, u32[]{:S(2)}) collective-permute-start(f32[8192]{0:T(1024)S(1)} %add.347), channel_id=1, source_target_pairs={{0,16},{8,24},{16,0},{24,8},{1,17},{9,25},{17,1},{25,9},{2,18},{10... | collective-permute-start | bytes 98312 | tf_op jit(solution)/shard_map/ppermute | solution.py:25
  47.2 1.9 collective-permute-done.18
  49.1 2.1 %collective-permute-done.19 = f32[8192]{0:T(1024)S(1)} collective-permute-done((f32[8192]{0:T(1024)S(1)}, f32[8192]{0:T(1024)S(1)}, u32[]{:S(2)}, u32[]{:S(2)}) %collective-permute-start.19) | collective-permute-done | bytes 32800 | tf_op jit(solution)/shard_map/ppermute | solution.py:25
  51.3 1.6 collective-permute-start.20
  52.9 2.9 %collective-permute-start.21 = (f32[8192]{0:T(1024)S(1)}, f32[8192]{0:T(1024)S(1)}, u32[]{:S(2)}, u32[]{:S(2)}) collective-permute-start(f32[8192]{0:T(1024)S(1)} %add_add_fusion.1), channel_id=1, source_target_pairs={{0,64},{32,96},{64,0},{96,32},{1,65},{33,97},{65,1},{97,33},{2,66}... | collective-permute-start | bytes 98312 | tf_op jit(solution)/shard_map/ppermute | solution.py:25
  60.4 5.6 %fusion.41 = f32[512,2]{0,1:T(2,128)S(1)} fusion(bf16[512,8192]{1,0:T(8,128)(2,1)} %get-tuple-element.110, bf16[1,8192]{1,0:T(2,128)(2,1)S(1)} %stack.52, bf16[1,8192]{1,0:T(2,128)(2,1)S(1)} %stack.51), kind=kOutput, calls=%fused_computation.88 | convolution fusion | flops 16842752 | bytes 8425472 | tf_op jit(solution)/shard_map/dot_general | solution.py:123
  66.2 2.0 collective-permute-start.24
  69.5 1.4 collective-permute-done.23
  71.9 62.8 %while.12 = (s32[]{:T(128)}, f32[8192]{0:T(1024)}, f32[512]{0:T(512)S(1)}, bf16[512,8192]{1,0:T(8,128)(2,1)}, s32[]{:T(128)}) while((s32[]{:T(128)}, f32[8192]{0:T(1024)}, f32[512]{0:T(512)S(1)}, bf16[512,8192]{1,0:T(8,128)(2,1)}, s32[]{:T(128)}) %tuple.48), condition=%wide.region_3.4_spmd, body=%wide.region_2.3_spmd.sunk | while | flops 33735168 | bytes 52025832 | solution.py:151
  72.0 4.7 %fusion.72 = f32[2,8192]{1,0:T(2,128)S(1)} fusion(bf16[512,8192]{1,0:T(8,128)(2,1)} %get-tuple-element.120, bf16[1,512]{1,0:T(2,128)(2,1)S(1)} %stack.59, bf16[1,512]{1,0:T(2,128)(2,1)S(1)} %stack.60), kind=kOutput, calls=%fused_computation.10.clone.1 | convolution fusion | flops 16781312 | bytes 8456192 | tf_op jit(solution)/shard_map/while/body/eval_jaxpr/dot_general | solution.py:118
  78.0 2.0 collective-permute-start.2
  81.3 1.9 collective-permute-done.1
  84.4 2.6 %collective-permute-start.4 = (f32[8192]{0:T(1024)S(1)}, f32[8192]{0:T(1024)S(1)}, u32[]{:S(2)}, u32[]{:S(2)}) collective-permute-start(f32[8192]{0:T(1024)S(1)} %add_add_fusion.4), channel_id=1, source_target_pairs={{0,96},{32,0},{64,32},{96,64},{1,97},{33,1},{65,33},{97,65},{2,98}... | collective-permute-start | bytes 98312 | tf_op jit(solution)/shard_map/while/body/eval_jaxpr/ppermute | solution.py:25
  88.6 3.9 %collective-permute-done.5 = f32[8192]{0:T(1024)S(1)} collective-permute-done((f32[8192]{0:T(1024)S(1)}, f32[8192]{0:T(1024)S(1)}, u32[]{:S(2)}, u32[]{:S(2)}) %collective-permute-start.5) | collective-permute-done | bytes 32800 | tf_op jit(solution)/shard_map/while/body/eval_jaxpr/ppermute | solution.py:25
  93.2 2.3 %convolution_bitcast_fusion.2 = f32[512,2]{0,1:T(2,128)S(1)} fusion(bf16[512,8192]{1,0:T(8,128)(2,1)S(1)} %copy-done.1, bf16[1,8192]{1,0:T(2,128)(2,1)S(1)} %stack.61, bf16[1,8192]{1,0:T(2,128)(2,1)S(1)} %stack.62), kind=kOutput, calls=%fused_computation.1.clone.1 | convolution fusion | flops 16842752 | bytes 8425472 | tf_op jit(solution)/shard_map/while/body/eval_jaxpr/dot_general | solution.py:123
  95.4 2.7 %collective-permute-start.7 = (f32[512]{0:T(512)S(1)}, f32[512]{0:T(512)S(1)}, u32[]{:S(2)}, u32[]{:S(2)}) collective-permute-start(f32[512]{0:T(512)S(1)} %bitcast.135), channel_id=1, source_target_pairs={{0,3},{1,0},{2,1},{3,2},{4,7},{5,4},{6,5},{7,6},{8,11},{9,8},{10,9... | collective-permute-start | bytes 6152 | tf_op jit(solution)/shard_map/while/body/eval_jaxpr/ppermute | solution.py:25
  99.5 3.7 %collective-permute-done.8 = f32[512]{0:T(512)S(1)} collective-permute-done((f32[512]{0:T(512)S(1)}, f32[512]{0:T(512)S(1)}, u32[]{:S(2)}, u32[]{:S(2)}) %collective-permute-start.8) | collective-permute-done | bytes 2080 | tf_op jit(solution)/shard_map/while/body/eval_jaxpr/ppermute | solution.py:25
  104.3 4.7 %fusion.72 = f32[2,8192]{1,0:T(2,128)S(1)} fusion(bf16[512,8192]{1,0:T(8,128)(2,1)} %get-tuple-element.120, bf16[1,512]{1,0:T(2,128)(2,1)S(1)} %stack.59, bf16[1,512]{1,0:T(2,128)(2,1)S(1)} %stack.60), kind=kOutput, calls=%fused_computation.10.clone.1 | convolution fusion | flops 16781312 | bytes 8456192 | tf_op jit(solution)/shard_map/while/body/eval_jaxpr/dot_general | solution.py:118
  110.4 1.7 collective-permute-start.1
  112.1 2.2 %collective-permute-start.2 = (f32[8192]{0:T(1024)S(1)}, f32[8192]{0:T(1024)S(1)}, u32[]{:S(2)}, u32[]{:S(2)}) collective-permute-start(f32[8192]{0:T(1024)S(1)} %add.526), channel_id=1, source_target_pairs={{0,16},{8,24},{16,0},{24,8},{1,17},{9,25},{17,1},{25,9},{2,18},{10... | collective-permute-start | bytes 98312 | tf_op jit(solution)/shard_map/while/body/eval_jaxpr/ppermute | solution.py:25
  115.5 2.0 collective-permute-done.2
  122.2 2.4 %collective-permute-done.5 = f32[8192]{0:T(1024)S(1)} collective-permute-done((f32[8192]{0:T(1024)S(1)}, f32[8192]{0:T(1024)S(1)}, u32[]{:S(2)}, u32[]{:S(2)}) %collective-permute-start.5) | collective-permute-done | bytes 32800 | tf_op jit(solution)/shard_map/while/body/eval_jaxpr/ppermute | solution.py:25
  126.1 2.3 %convolution_bitcast_fusion.2 = f32[512,2]{0,1:T(2,128)S(1)} fusion(bf16[512,8192]{1,0:T(8,128)(2,1)S(1)} %copy-done.1, bf16[1,8192]{1,0:T(2,128)(2,1)S(1)} %stack.61, bf16[1,8192]{1,0:T(2,128)(2,1)S(1)} %stack.62), kind=kOutput, calls=%fused_computation.1.clone.1 | convolution fusion | flops 16842752 | bytes 8425472 | tf_op jit(solution)/shard_map/while/body/eval_jaxpr/dot_general | solution.py:123
  132.0 1.6 collective-permute-done.8
  134.7 11.2 %multiply_convert_fusion = (bf16[512,8192]{1,0:T(8,128)(2,1)S(1)}, bf16[512,8192]{1,0:T(8,128)(2,1)}) fusion(f32[512,8192]{1,0:T(8,128)} %get-tuple-element.29, f32[512]{0:T(512)S(1)} %bitcast.147, f32[512]{0:T(512)S(1)} %get-tuple-element.34, f32[8192]{0:T(1024)} %get-tuple-element.33), kind=kLoop, calls=%fused_computation.18 | loop fusion | flops 37748736 | bytes 33591296 | tf_op jit(solution)/shard_map/convert_element_type | solution.py:157
  145.8 2.4 %fusion.51 = (bf16[512,256]{1,0:T(8,128)(2,1)S(1)}, f32[512,256]{1,0:T(8,128)S(1)}) fusion(bf16[512,8192]{1,0:T(8,128)(2,1)S(1)} %get-tuple-element.53, bf16[256,8192]{1,0:T(8,128)(2,1)S(1)} %copy-done.4), kind=kOutput, calls=%fused_computation.114 | convolution fusion | flops 2147614720 | bytes 13369344 | tf_op jit(solution)/shard_map/dot_general | solution.py:162
  149.1 2.6 %collective-permute-start.34 = (bf16[512,256]{1,0:T(8,128)(2,1)S(1)}, bf16[512,256]{1,0:T(8,128)(2,1)S(1)}, u32[]{:S(2)}, u32[]{:S(2)}) collective-permute-start(bf16[512,256]{1,0:T(8,128)(2,1)S(1)} %get-tuple-element.72), channel_id=1, source_target_pairs={{0,2},{1,3},{2,0},{3,1},{4,6},{5,7},{6,4},{7,5},{8,10},{9,11},{10,... | collective-permute-start | bytes 786440 | tf_op jit(solution)/shard_map/ppermute | solution.py:25
  152.1 1.9 fusion.11
  154.7 1.7 collective-permute-done.33
  156.4 2.8 %collective-permute-done.34 = bf16[512,256]{1,0:T(8,128)(2,1)S(1)} collective-permute-done((bf16[512,256]{1,0:T(8,128)(2,1)S(1)}, bf16[512,256]{1,0:T(8,128)(2,1)S(1)}, u32[]{:S(2)}, u32[]{:S(2)}) %collective-permute-start.34) | collective-permute-done | bytes 262176 | tf_op jit(solution)/shard_map/ppermute | solution.py:25
  165.7 2.3 %collective-permute-start.37 = (bf16[4,8,2560]{2,1,0:T(8,128)(2,1)S(1)}, bf16[4,8,2560]{2,1,0:T(8,128)(2,1)S(1)}, u32[]{:S(2)}, u32[]{:S(2)}) collective-permute-start(bf16[4,8,2560]{2,1,0:T(8,128)(2,1)S(1)} %get-tuple-element.58), channel_id=1, source_target_pairs={{0,8},{8,16},{16,24},{24,0},{1,9},{9,17},{17,25},{25,1},{2,10},{10... | collective-permute-start | bytes 491528 | tf_op jit(solution)/shard_map/ppermute | solution.py:25
  168.9 2.7 %bitcast_add_fusion = f32[4,4,8,6144]{3,2,1,0:T(8,128)S(1)} fusion(bf16[4,4,8,6144]{3,2,1,0:T(8,128)(2,1)} %collective-permute-done.26, f32[4,4,2,8,6144]{4,3,2,1,0:T(8,128)} %copy-done.2, s32[]{:T(128)S(6)} %select_n.148), kind=kLoop, calls=%fused_computation.27 | loop fusion | flops 1572864 | bytes 7864324 | tf_op jit(solution)/shard_map/add | solution.py:50
  171.8 2.4 %collective-permute-start.27 = (bf16[4,8,6144]{2,1,0:T(8,128)(2,1)S(1)}, bf16[4,8,6144]{2,1,0:T(8,128)(2,1)S(1)}, u32[]{:S(2)}, u32[]{:S(2)}) collective-permute-start(bf16[4,8,6144]{2,1,0:T(8,128)(2,1)S(1)} %get-tuple-element.55), channel_id=1, source_target_pairs={{0,8},{8,16},{16,24},{24,0},{1,9},{9,17},{17,25},{25,1},{2,10},{10... | collective-permute-start | bytes 1179656 | tf_op jit(solution)/shard_map/ppermute | solution.py:25
  174.2 2.3 %collective-permute-start.28 = (bf16[4,8,6144]{2,1,0:T(8,128)(2,1)S(1)}, bf16[4,8,6144]{2,1,0:T(8,128)(2,1)S(1)}, u32[]{:S(2)}, u32[]{:S(2)}) collective-permute-start(bf16[4,8,6144]{2,1,0:T(8,128)(2,1)S(1)} %get-tuple-element.57), channel_id=1, source_target_pairs={{0,16},{8,24},{16,0},{24,8},{1,17},{9,25},{17,1},{25,9},{2,18},{10... | collective-permute-start | bytes 1179656 | tf_op jit(solution)/shard_map/ppermute | solution.py:25
  176.6 3.2 %collective-permute-done.39 = bf16[4,8,2560]{2,1,0:T(8,128)(2,1)S(1)} collective-permute-done((bf16[4,8,2560]{2,1,0:T(8,128)(2,1)S(1)}, bf16[4,8,2560]{2,1,0:T(8,128)(2,1)S(1)}, u32[]{:S(2)}, u32[]{:S(2)}) %collective-permute-start.39) | collective-permute-done | bytes 163872 | tf_op jit(solution)/shard_map/ppermute | solution.py:25
  180.4 2.4 %collective-permute-start.41 = (bf16[8,2560]{1,0:T(8,128)(2,1)S(1)}, bf16[8,2560]{1,0:T(8,128)(2,1)S(1)}, u32[]{:S(2)}, u32[]{:S(2)}) collective-permute-start(bf16[8,2560]{1,0:T(8,128)(2,1)S(1)} %get-tuple-element.69), channel_id=1, source_target_pairs={{0,64},{32,96},{64,0},{96,32},{1,65},{33,97},{65,1},{97,33},{2,66}... | collective-permute-start | bytes 122888 | tf_op jit(solution)/shard_map/ppermute | solution.py:25
  182.8 9.3 %collective-permute-done.27 = bf16[4,8,6144]{2,1,0:T(8,128)(2,1)S(1)} collective-permute-done((bf16[4,8,6144]{2,1,0:T(8,128)(2,1)S(1)}, bf16[4,8,6144]{2,1,0:T(8,128)(2,1)S(1)}, u32[]{:S(2)}, u32[]{:S(2)}) %collective-permute-start.27) | collective-permute-done | bytes 393248 | tf_op jit(solution)/shard_map/ppermute | solution.py:25
  193.6 2.0 collective-permute-done.29
  196.3 2.4 %collective-permute-start.31 = (bf16[8,6144]{1,0:T(8,128)(2,1)S(1)}, bf16[8,6144]{1,0:T(8,128)(2,1)S(1)}, u32[]{:S(2)}, u32[]{:S(2)}) collective-permute-start(bf16[8,6144]{1,0:T(8,128)(2,1)S(1)} %get-tuple-element.63), channel_id=1, source_target_pairs={{0,64},{32,96},{64,0},{96,32},{1,65},{33,97},{65,1},{97,33},{2,66}... | collective-permute-start | bytes 294920 | tf_op jit(solution)/shard_map/ppermute | solution.py:25
  200.3 3.2 %collective-permute-done.30 = bf16[8,6144]{1,0:T(8,128)(2,1)S(1)} collective-permute-done((bf16[8,6144]{1,0:T(8,128)(2,1)S(1)}, bf16[8,6144]{1,0:T(8,128)(2,1)S(1)}, u32[]{:S(2)}, u32[]{:S(2)}) %collective-permute-start.30) | collective-permute-done | bytes 98336 | tf_op jit(solution)/shard_map/ppermute | solution.py:25
  (147 shorter events, 54.9 us)
Async XLA Ops:
  3.1 12.6 %collective-permute-start.10 = (f32[128,256]{1,0:T(8,128)S(1)}, f32[128,256]{1,0:T(8,128)S(1)}, u32[]{:S(2)}, u32[]{:S(2)}) collective-permute-start(f32[128,256]{1,0:T(8,128)S(1)} %get-tuple-element.64), channel_id=1, source_target_pairs={{0,1},{1,2},{2,3},{3,0},{4,5},{5,6},{6,7},{7,4},{8,9},{9,10},{10,1... | collective-permute-start | bytes 393224 | tf_op jit(solution)/shard_map/ppermute | solution.py:25
  5.1 10.6 %collective-permute-start.11 = (f32[128,256]{1,0:T(8,128)S(1)}, f32[128,256]{1,0:T(8,128)S(1)}, u32[]{:S(2)}, u32[]{:S(2)}) collective-permute-start(f32[128,256]{1,0:T(8,128)S(1)} %get-tuple-element.66), channel_id=1, source_target_pairs={{0,2},{1,3},{2,0},{3,1},{4,6},{5,7},{6,4},{7,5},{8,10},{9,11},{10,... | collective-permute-start | bytes 393224 | tf_op jit(solution)/shard_map/ppermute | solution.py:25
  8.7 7.0 %collective-permute-start.12 = (f32[128,256]{1,0:T(8,128)S(1)}, f32[128,256]{1,0:T(8,128)S(1)}, u32[]{:S(2)}, u32[]{:S(2)}) collective-permute-start(f32[128,256]{1,0:T(8,128)S(1)} %get-tuple-element.65), channel_id=1, source_target_pairs={{0,3},{1,0},{2,1},{3,2},{4,7},{5,4},{6,5},{7,6},{8,11},{9,8},{10,9... | collective-permute-start | bytes 393224 | tf_op jit(solution)/shard_map/ppermute | solution.py:25
  15.8 7.6 %collective-permute-start.14 = (f32[128,256]{1,0:T(8,128)S(1)}, f32[128,256]{1,0:T(8,128)S(1)}, u32[]{:S(2)}, u32[]{:S(2)}) collective-permute-start(f32[128,256]{1,0:T(8,128)S(1)} %fusion.32), channel_id=1, source_target_pairs={{0,2},{1,3},{2,0},{3,1},{4,6},{5,7},{6,4},{7,5},{8,10},{9,11},{10,... | collective-permute-start | bytes 393224 | tf_op jit(solution)/shard_map/ppermute | solution.py:25
  17.1 6.4 %collective-permute-start.15 = (f32[128,256]{1,0:T(8,128)S(1)}, f32[128,256]{1,0:T(8,128)S(1)}, u32[]{:S(2)}, u32[]{:S(2)}) collective-permute-start(f32[128,256]{1,0:T(8,128)S(1)} %fusion.32), channel_id=1, source_target_pairs={{0,3},{1,0},{2,1},{3,2},{4,7},{5,4},{6,5},{7,6},{8,11},{9,8},{10,9... | collective-permute-start | bytes 393224 | tf_op jit(solution)/shard_map/ppermute | solution.py:25
  19.6 6.2 %collective-permute-start.13 = (f32[128,256]{1,0:T(8,128)S(1)}, f32[128,256]{1,0:T(8,128)S(1)}, u32[]{:S(2)}, u32[]{:S(2)}) collective-permute-start(f32[128,256]{1,0:T(8,128)S(1)} %fusion.32), channel_id=1, source_target_pairs={{0,1},{1,2},{2,3},{3,0},{4,5},{5,6},{6,7},{7,4},{8,9},{9,10},{10,1... | collective-permute-start | bytes 393224 | tf_op jit(solution)/shard_map/ppermute | solution.py:25
  43.2 4.0 %collective-permute-start.17 = (f32[8192]{0:T(1024)S(1)}, f32[8192]{0:T(1024)S(1)}, u32[]{:S(2)}, u32[]{:S(2)}) collective-permute-start(f32[8192]{0:T(1024)S(1)} %add.347), channel_id=1, source_target_pairs={{0,8},{8,16},{16,24},{24,0},{1,9},{9,17},{17,25},{25,1},{2,10},{10... | collective-permute-start | bytes 98312 | tf_op jit(solution)/shard_map/ppermute | solution.py:25
  43.7 5.4 %collective-permute-start.18 = (f32[8192]{0:T(1024)S(1)}, f32[8192]{0:T(1024)S(1)}, u32[]{:S(2)}, u32[]{:S(2)}) collective-permute-start(f32[8192]{0:T(1024)S(1)} %add.347), channel_id=1, source_target_pairs={{0,16},{8,24},{16,0},{24,8},{1,17},{9,25},{17,1},{25,9},{2,18},{10... | collective-permute-start | bytes 98312 | tf_op jit(solution)/shard_map/ppermute | solution.py:25
  46.1 5.1 %collective-permute-start.19 = (f32[8192]{0:T(1024)S(1)}, f32[8192]{0:T(1024)S(1)}, u32[]{:S(2)}, u32[]{:S(2)}) collective-permute-start(f32[8192]{0:T(1024)S(1)} %add.347), channel_id=1, source_target_pairs={{0,24},{8,0},{16,8},{24,16},{1,25},{9,1},{17,9},{25,17},{2,26},{10... | collective-permute-start | bytes 98312 | tf_op jit(solution)/shard_map/ppermute | solution.py:25
  51.3 7.0 %collective-permute-start.20 = (f32[8192]{0:T(1024)S(1)}, f32[8192]{0:T(1024)S(1)}, u32[]{:S(2)}, u32[]{:S(2)}) collective-permute-start(f32[8192]{0:T(1024)S(1)} %add_add_fusion.1), channel_id=1, source_target_pairs={{0,32},{32,64},{64,96},{96,0},{1,33},{33,65},{65,97},{97,1},{2,34}... | collective-permute-start | bytes 98312 | tf_op jit(solution)/shard_map/ppermute | solution.py:25
  52.9 5.4 %collective-permute-start.21 = (f32[8192]{0:T(1024)S(1)}, f32[8192]{0:T(1024)S(1)}, u32[]{:S(2)}, u32[]{:S(2)}) collective-permute-start(f32[8192]{0:T(1024)S(1)} %add_add_fusion.1), channel_id=1, source_target_pairs={{0,64},{32,96},{64,0},{96,32},{1,65},{33,97},{65,1},{97,33},{2,66}... | collective-permute-start | bytes 98312 | tf_op jit(solution)/shard_map/ppermute | solution.py:25
  55.8 3.9 %collective-permute-start.22 = (f32[8192]{0:T(1024)S(1)}, f32[8192]{0:T(1024)S(1)}, u32[]{:S(2)}, u32[]{:S(2)}) collective-permute-start(f32[8192]{0:T(1024)S(1)} %add_add_fusion.1), channel_id=1, source_target_pairs={{0,96},{32,0},{64,32},{96,64},{1,97},{33,1},{65,33},{97,65},{2,98}... | collective-permute-start | bytes 98312 | tf_op jit(solution)/shard_map/ppermute | solution.py:25
  66.1 4.9 %collective-permute-start.23 = (f32[2,512]{1,0:T(2,128)S(1)}, f32[2,512]{1,0:T(2,128)S(1)}, u32[]{:S(2)}, u32[]{:S(2)}) collective-permute-start(f32[2,512]{1,0:T(2,128)S(1)} %pad_maximum_fusion.3), channel_id=1, source_target_pairs={{0,1},{1,2},{2,3},{3,0},{4,5},{5,6},{6,7},{7,4},{8,9},{9,10},{10,1... | collective-permute-start | bytes 12296 | tf_op jit(solution)/shard_map/ppermute | solution.py:25
  66.2 5.2 %collective-permute-start.24 = (f32[2,512]{1,0:T(2,128)S(1)}, f32[2,512]{1,0:T(2,128)S(1)}, u32[]{:S(2)}, u32[]{:S(2)}) collective-permute-start(f32[2,512]{1,0:T(2,128)S(1)} %pad_maximum_fusion.3), channel_id=1, source_target_pairs={{0,2},{1,3},{2,0},{3,1},{4,6},{5,7},{6,4},{7,5},{8,10},{9,11},{10,... | collective-permute-start | bytes 12296 | tf_op jit(solution)/shard_map/ppermute | solution.py:25
  68.2 3.7 %collective-permute-start.25 = (f32[2,512]{1,0:T(2,128)S(1)}, f32[2,512]{1,0:T(2,128)S(1)}, u32[]{:S(2)}, u32[]{:S(2)}) collective-permute-start(f32[2,512]{1,0:T(2,128)S(1)} %pad_maximum_fusion.3), channel_id=1, source_target_pairs={{0,3},{1,0},{2,1},{3,2},{4,7},{5,4},{6,5},{7,6},{8,11},{9,8},{10,9... | collective-permute-start | bytes 12296 | tf_op jit(solution)/shard_map/ppermute | solution.py:25
  78.0 5.1 %collective-permute-start.1 = (f32[8192]{0:T(1024)S(1)}, f32[8192]{0:T(1024)S(1)}, u32[]{:S(2)}, u32[]{:S(2)}) collective-permute-start(f32[8192]{0:T(1024)S(1)} %add.526), channel_id=1, source_target_pairs={{0,24},{8,0},{16,8},{24,16},{1,25},{9,1},{17,9},{25,17},{2,26},{10... | collective-permute-start | bytes 98312 | tf_op jit(solution)/shard_map/while/body/eval_jaxpr/ppermute | solution.py:25
  78.0 5.5 %collective-permute-start.2 = (f32[8192]{0:T(1024)S(1)}, f32[8192]{0:T(1024)S(1)}, u32[]{:S(2)}, u32[]{:S(2)}) collective-permute-start(f32[8192]{0:T(1024)S(1)} %add.526), channel_id=1, source_target_pairs={{0,16},{8,24},{16,0},{24,8},{1,17},{9,25},{17,1},{25,9},{2,18},{10... | collective-permute-start | bytes 98312 | tf_op jit(solution)/shard_map/while/body/eval_jaxpr/ppermute | solution.py:25
  80.1 4.3 %collective-permute-start.3 = (f32[8192]{0:T(1024)S(1)}, f32[8192]{0:T(1024)S(1)}, u32[]{:S(2)}, u32[]{:S(2)}) collective-permute-start(f32[8192]{0:T(1024)S(1)} %add.526), channel_id=1, source_target_pairs={{0,8},{8,16},{16,24},{24,0},{1,9},{9,17},{17,25},{25,1},{2,10},{10... | collective-permute-start | bytes 98312 | tf_op jit(solution)/shard_map/while/body/eval_jaxpr/ppermute | solution.py:25
  84.4 4.2 %collective-permute-start.4 = (f32[8192]{0:T(1024)S(1)}, f32[8192]{0:T(1024)S(1)}, u32[]{:S(2)}, u32[]{:S(2)}) collective-permute-start(f32[8192]{0:T(1024)S(1)} %add_add_fusion.4), channel_id=1, source_target_pairs={{0,96},{32,0},{64,32},{96,64},{1,97},{33,1},{65,33},{97,65},{2,98}... | collective-permute-start | bytes 98312 | tf_op jit(solution)/shard_map/while/body/eval_jaxpr/ppermute | solution.py:25
  87.0 5.5 %collective-permute-start.5 = (f32[8192]{0:T(1024)S(1)}, f32[8192]{0:T(1024)S(1)}, u32[]{:S(2)}, u32[]{:S(2)}) collective-permute-start(f32[8192]{0:T(1024)S(1)} %add_add_fusion.4), channel_id=1, source_target_pairs={{0,64},{32,96},{64,0},{96,32},{1,65},{33,97},{65,1},{97,33},{2,66}... | collective-permute-start | bytes 98312 | tf_op jit(solution)/shard_map/while/body/eval_jaxpr/ppermute | solution.py:25
  87.0 5.5 %collective-permute-start.6 = (f32[8192]{0:T(1024)S(1)}, f32[8192]{0:T(1024)S(1)}, u32[]{:S(2)}, u32[]{:S(2)}) collective-permute-start(f32[8192]{0:T(1024)S(1)} %add_add_fusion.4), channel_id=1, source_target_pairs={{0,32},{32,64},{64,96},{96,0},{1,33},{33,65},{65,97},{97,1},{2,34}... | collective-permute-start | bytes 98312 | tf_op jit(solution)/shard_map/while/body/eval_jaxpr/ppermute | solution.py:25
  95.4 4.1 %collective-permute-start.7 = (f32[512]{0:T(512)S(1)}, f32[512]{0:T(512)S(1)}, u32[]{:S(2)}, u32[]{:S(2)}) collective-permute-start(f32[512]{0:T(512)S(1)} %bitcast.135), channel_id=1, source_target_pairs={{0,3},{1,0},{2,1},{3,2},{4,7},{5,4},{6,5},{7,6},{8,11},{9,8},{10,9... | collective-permute-start | bytes 6152 | tf_op jit(solution)/shard_map/while/body/eval_jaxpr/ppermute | solution.py:25
  98.1 5.1 %collective-permute-start.8 = (f32[512]{0:T(512)S(1)}, f32[512]{0:T(512)S(1)}, u32[]{:S(2)}, u32[]{:S(2)}) collective-permute-start(f32[512]{0:T(512)S(1)} %bitcast.136), channel_id=1, source_target_pairs={{0,2},{1,3},{2,0},{3,1},{4,6},{5,7},{6,4},{7,5},{8,10},{9,11},{10,... | collective-permute-start | bytes 6152 | tf_op jit(solution)/shard_map/while/body/eval_jaxpr/ppermute | solution.py:25
  99.5 4.8 %collective-permute-start.9 = (f32[512]{0:T(512)S(1)}, f32[512]{0:T(512)S(1)}, u32[]{:S(2)}, u32[]{:S(2)}) collective-permute-start(f32[512]{0:T(512)S(1)} %bitcast.137), channel_id=1, source_target_pairs={{0,1},{1,2},{2,3},{3,0},{4,5},{5,6},{6,7},{7,4},{8,9},{9,10},{10,1... | collective-permute-start | bytes 6152 | tf_op jit(solution)/shard_map/while/body/eval_jaxpr/ppermute | solution.py:25
  110.4 5.1 %collective-permute-start.1 = (f32[8192]{0:T(1024)S(1)}, f32[8192]{0:T(1024)S(1)}, u32[]{:S(2)}, u32[]{:S(2)}) collective-permute-start(f32[8192]{0:T(1024)S(1)} %add.526), channel_id=1, source_target_pairs={{0,24},{8,0},{16,8},{24,16},{1,25},{9,1},{17,9},{25,17},{2,26},{10... | collective-permute-start | bytes 98312 | tf_op jit(solution)/shard_map/while/body/eval_jaxpr/ppermute | solution.py:25
  112.1 5.4 %collective-permute-start.2 = (f32[8192]{0:T(1024)S(1)}, f32[8192]{0:T(1024)S(1)}, u32[]{:S(2)}, u32[]{:S(2)}) collective-permute-start(f32[8192]{0:T(1024)S(1)} %add.526), channel_id=1, source_target_pairs={{0,16},{8,24},{16,0},{24,8},{1,17},{9,25},{17,1},{25,9},{2,18},{10... | collective-permute-start | bytes 98312 | tf_op jit(solution)/shard_map/while/body/eval_jaxpr/ppermute | solution.py:25
  114.3 3.9 %collective-permute-start.3 = (f32[8192]{0:T(1024)S(1)}, f32[8192]{0:T(1024)S(1)}, u32[]{:S(2)}, u32[]{:S(2)}) collective-permute-start(f32[8192]{0:T(1024)S(1)} %add.526), channel_id=1, source_target_pairs={{0,8},{8,16},{16,24},{24,0},{1,9},{9,17},{17,25},{25,1},{2,10},{10... | collective-permute-start | bytes 98312 | tf_op jit(solution)/shard_map/while/body/eval_jaxpr/ppermute | solution.py:25
  118.2 4.0 %collective-permute-start.4 = (f32[8192]{0:T(1024)S(1)}, f32[8192]{0:T(1024)S(1)}, u32[]{:S(2)}, u32[]{:S(2)}) collective-permute-start(f32[8192]{0:T(1024)S(1)} %add_add_fusion.4), channel_id=1, source_target_pairs={{0,96},{32,0},{64,32},{96,64},{1,97},{33,1},{65,33},{97,65},{2,98}... | collective-permute-start | bytes 98312 | tf_op jit(solution)/shard_map/while/body/eval_jaxpr/ppermute | solution.py:25
  119.1 5.4 %collective-permute-start.5 = (f32[8192]{0:T(1024)S(1)}, f32[8192]{0:T(1024)S(1)}, u32[]{:S(2)}, u32[]{:S(2)}) collective-permute-start(f32[8192]{0:T(1024)S(1)} %add_add_fusion.4), channel_id=1, source_target_pairs={{0,64},{32,96},{64,0},{96,32},{1,65},{33,97},{65,1},{97,33},{2,66}... | collective-permute-start | bytes 98312 | tf_op jit(solution)/shard_map/while/body/eval_jaxpr/ppermute | solution.py:25
  120.3 5.1 %collective-permute-start.6 = (f32[8192]{0:T(1024)S(1)}, f32[8192]{0:T(1024)S(1)}, u32[]{:S(2)}, u32[]{:S(2)}) collective-permute-start(f32[8192]{0:T(1024)S(1)} %add_add_fusion.4), channel_id=1, source_target_pairs={{0,32},{32,64},{64,96},{96,0},{1,33},{33,65},{65,97},{97,1},{2,34}... | collective-permute-start | bytes 98312 | tf_op jit(solution)/shard_map/while/body/eval_jaxpr/ppermute | solution.py:25
  128.4 5.2 %collective-permute-start.8 = (f32[512]{0:T(512)S(1)}, f32[512]{0:T(512)S(1)}, u32[]{:S(2)}, u32[]{:S(2)}) collective-permute-start(f32[512]{0:T(512)S(1)} %bitcast.136), channel_id=1, source_target_pairs={{0,2},{1,3},{2,0},{3,1},{4,6},{5,7},{6,4},{7,5},{8,10},{9,11},{10,... | collective-permute-start | bytes 6152 | tf_op jit(solution)/shard_map/while/body/eval_jaxpr/ppermute | solution.py:25
  129.4 5.3 %collective-permute-start.9 = (f32[512]{0:T(512)S(1)}, f32[512]{0:T(512)S(1)}, u32[]{:S(2)}, u32[]{:S(2)}) collective-permute-start(f32[512]{0:T(512)S(1)} %bitcast.137), channel_id=1, source_target_pairs={{0,1},{1,2},{2,3},{3,0},{4,5},{5,6},{6,7},{7,4},{8,9},{9,10},{10,1... | collective-permute-start | bytes 6152 | tf_op jit(solution)/shard_map/while/body/eval_jaxpr/ppermute | solution.py:25
  148.2 8.2 %collective-permute-start.33 = (bf16[512,256]{1,0:T(8,128)(2,1)S(1)}, bf16[512,256]{1,0:T(8,128)(2,1)S(1)}, u32[]{:S(2)}, u32[]{:S(2)}) collective-permute-start(bf16[512,256]{1,0:T(8,128)(2,1)S(1)} %get-tuple-element.72), channel_id=1, source_target_pairs={{0,1},{1,2},{2,3},{3,0},{4,5},{5,6},{6,7},{7,4},{8,9},{9,10},{10,1... | collective-permute-start | bytes 786440 | tf_op jit(solution)/shard_map/ppermute | solution.py:25
  149.1 10.1 %collective-permute-start.34 = (bf16[512,256]{1,0:T(8,128)(2,1)S(1)}, bf16[512,256]{1,0:T(8,128)(2,1)S(1)}, u32[]{:S(2)}, u32[]{:S(2)}) collective-permute-start(bf16[512,256]{1,0:T(8,128)(2,1)S(1)} %get-tuple-element.72), channel_id=1, source_target_pairs={{0,2},{1,3},{2,0},{3,1},{4,6},{5,7},{6,4},{7,5},{8,10},{9,11},{10,... | collective-permute-start | bytes 786440 | tf_op jit(solution)/shard_map/ppermute | solution.py:25
  151.8 8.1 %collective-permute-start.35 = (bf16[512,256]{1,0:T(8,128)(2,1)S(1)}, bf16[512,256]{1,0:T(8,128)(2,1)S(1)}, u32[]{:S(2)}, u32[]{:S(2)}) collective-permute-start(bf16[512,256]{1,0:T(8,128)(2,1)S(1)} %get-tuple-element.72), channel_id=1, source_target_pairs={{0,3},{1,0},{2,1},{3,2},{4,7},{5,4},{6,5},{7,6},{8,11},{9,8},{10,9... | collective-permute-start | bytes 786440 | tf_op jit(solution)/shard_map/ppermute | solution.py:25
  163.3 5.6 %collective-permute-start.26 = (bf16[4,4,8,6144]{3,2,1,0:T(8,128)(2,1)}, bf16[4,4,8,6144]{3,2,1,0:T(8,128)(2,1)}, u32[]{:S(2)}, u32[]{:S(2)}) collective-permute-start(bf16[4,4,8,6144]{3,2,1,0:T(8,128)(2,1)} %fusion.14), channel_id=1, source_target_pairs={{0,4},{4,0},{1,5},{5,1},{2,6},{6,2},{3,7},{7,3},{8,12},{12,8},{9,1... | collective-permute-start | bytes 4718600 | tf_op jit(solution)/shard_map/ppermute | solution.py:25
  165.7 10.9 %collective-permute-start.37 = (bf16[4,8,2560]{2,1,0:T(8,128)(2,1)S(1)}, bf16[4,8,2560]{2,1,0:T(8,128)(2,1)S(1)}, u32[]{:S(2)}, u32[]{:S(2)}) collective-permute-start(bf16[4,8,2560]{2,1,0:T(8,128)(2,1)S(1)} %get-tuple-element.58), channel_id=1, source_target_pairs={{0,8},{8,16},{16,24},{24,0},{1,9},{9,17},{17,25},{25,1},{2,10},{10... | collective-permute-start | bytes 491528 | tf_op jit(solution)/shard_map/ppermute | solution.py:25
  168.0 8.6 %collective-permute-start.38 = (bf16[4,8,2560]{2,1,0:T(8,128)(2,1)S(1)}, bf16[4,8,2560]{2,1,0:T(8,128)(2,1)S(1)}, u32[]{:S(2)}, u32[]{:S(2)}) collective-permute-start(bf16[4,8,2560]{2,1,0:T(8,128)(2,1)S(1)} %get-tuple-element.60), channel_id=1, source_target_pairs={{0,16},{8,24},{16,0},{24,8},{1,17},{9,25},{17,1},{25,9},{2,18},{10... | collective-permute-start | bytes 491528 | tf_op jit(solution)/shard_map/ppermute | solution.py:25
  168.0 11.8 %collective-permute-start.39 = (bf16[4,8,2560]{2,1,0:T(8,128)(2,1)S(1)}, bf16[4,8,2560]{2,1,0:T(8,128)(2,1)S(1)}, u32[]{:S(2)}, u32[]{:S(2)}) collective-permute-start(bf16[4,8,2560]{2,1,0:T(8,128)(2,1)S(1)} %get-tuple-element.59), channel_id=1, source_target_pairs={{0,24},{8,0},{16,8},{24,16},{1,25},{9,1},{17,9},{25,17},{2,26},{10... | collective-permute-start | bytes 491528 | tf_op jit(solution)/shard_map/ppermute | solution.py:25
  171.8 20.3 %collective-permute-start.27 = (bf16[4,8,6144]{2,1,0:T(8,128)(2,1)S(1)}, bf16[4,8,6144]{2,1,0:T(8,128)(2,1)S(1)}, u32[]{:S(2)}, u32[]{:S(2)}) collective-permute-start(bf16[4,8,6144]{2,1,0:T(8,128)(2,1)S(1)} %get-tuple-element.55), channel_id=1, source_target_pairs={{0,8},{8,16},{16,24},{24,0},{1,9},{9,17},{17,25},{25,1},{2,10},{10... | collective-permute-start | bytes 1179656 | tf_op jit(solution)/shard_map/ppermute | solution.py:25
  174.2 19.4 %collective-permute-start.28 = (bf16[4,8,6144]{2,1,0:T(8,128)(2,1)S(1)}, bf16[4,8,6144]{2,1,0:T(8,128)(2,1)S(1)}, u32[]{:S(2)}, u32[]{:S(2)}) collective-permute-start(bf16[4,8,6144]{2,1,0:T(8,128)(2,1)S(1)} %get-tuple-element.57), channel_id=1, source_target_pairs={{0,16},{8,24},{16,0},{24,8},{1,17},{9,25},{17,1},{25,9},{2,18},{10... | collective-permute-start | bytes 1179656 | tf_op jit(solution)/shard_map/ppermute | solution.py:25
  176.5 19.0 %collective-permute-start.29 = (bf16[4,8,6144]{2,1,0:T(8,128)(2,1)S(1)}, bf16[4,8,6144]{2,1,0:T(8,128)(2,1)S(1)}, u32[]{:S(2)}, u32[]{:S(2)}) collective-permute-start(bf16[4,8,6144]{2,1,0:T(8,128)(2,1)S(1)} %get-tuple-element.56), channel_id=1, source_target_pairs={{0,24},{8,0},{16,8},{24,16},{1,25},{9,1},{17,9},{25,17},{2,26},{10... | collective-permute-start | bytes 1179656 | tf_op jit(solution)/shard_map/ppermute | solution.py:25
  179.9 18.8 %collective-permute-start.40 = (bf16[8,2560]{1,0:T(8,128)(2,1)S(1)}, bf16[8,2560]{1,0:T(8,128)(2,1)S(1)}, u32[]{:S(2)}, u32[]{:S(2)}) collective-permute-start(bf16[8,2560]{1,0:T(8,128)(2,1)S(1)} %get-tuple-element.67), channel_id=1, source_target_pairs={{0,32},{32,64},{64,96},{96,0},{1,33},{33,65},{65,97},{97,1},{2,34}... | collective-permute-start | bytes 122888 | tf_op jit(solution)/shard_map/ppermute | solution.py:25
  180.4 19.3 %collective-permute-start.41 = (bf16[8,2560]{1,0:T(8,128)(2,1)S(1)}, bf16[8,2560]{1,0:T(8,128)(2,1)S(1)}, u32[]{:S(2)}, u32[]{:S(2)}) collective-permute-start(bf16[8,2560]{1,0:T(8,128)(2,1)S(1)} %get-tuple-element.69), channel_id=1, source_target_pairs={{0,64},{32,96},{64,0},{96,32},{1,65},{33,97},{65,1},{97,33},{2,66}... | collective-permute-start | bytes 122888 | tf_op jit(solution)/shard_map/ppermute | solution.py:25
  192.1 7.6 %collective-permute-start.42 = (bf16[8,2560]{1,0:T(8,128)(2,1)S(1)}, bf16[8,2560]{1,0:T(8,128)(2,1)S(1)}, u32[]{:S(2)}, u32[]{:S(2)}) collective-permute-start(bf16[8,2560]{1,0:T(8,128)(2,1)S(1)} %get-tuple-element.68), channel_id=1, source_target_pairs={{0,96},{32,0},{64,32},{96,64},{1,97},{33,1},{65,33},{97,65},{2,98}... | collective-permute-start | bytes 122888 | tf_op jit(solution)/shard_map/ppermute | solution.py:25
  195.8 7.8 %collective-permute-start.30 = (bf16[8,6144]{1,0:T(8,128)(2,1)S(1)}, bf16[8,6144]{1,0:T(8,128)(2,1)S(1)}, u32[]{:S(2)}, u32[]{:S(2)}) collective-permute-start(bf16[8,6144]{1,0:T(8,128)(2,1)S(1)} %get-tuple-element.61), channel_id=1, source_target_pairs={{0,32},{32,64},{64,96},{96,0},{1,33},{33,65},{65,97},{97,1},{2,34}... | collective-permute-start | bytes 294920 | tf_op jit(solution)/shard_map/ppermute | solution.py:25
  196.3 7.2 %collective-permute-start.31 = (bf16[8,6144]{1,0:T(8,128)(2,1)S(1)}, bf16[8,6144]{1,0:T(8,128)(2,1)S(1)}, u32[]{:S(2)}, u32[]{:S(2)}) collective-permute-start(bf16[8,6144]{1,0:T(8,128)(2,1)S(1)} %get-tuple-element.63), channel_id=1, source_target_pairs={{0,64},{32,96},{64,0},{96,32},{1,65},{33,97},{65,1},{97,33},{2,66}... | collective-permute-start | bytes 294920 | tf_op jit(solution)/shard_map/ppermute | solution.py:25
  198.7 5.4 %collective-permute-start.32 = (bf16[8,6144]{1,0:T(8,128)(2,1)S(1)}, bf16[8,6144]{1,0:T(8,128)(2,1)S(1)}, u32[]{:S(2)}, u32[]{:S(2)}) collective-permute-start(bf16[8,6144]{1,0:T(8,128)(2,1)S(1)} %get-tuple-element.62), channel_id=1, source_target_pairs={{0,96},{32,0},{64,32},{96,64},{1,97},{33,1},{65,33},{97,65},{2,98}... | collective-permute-start | bytes 294920 | tf_op jit(solution)/shard_map/ppermute | solution.py:25
  (12 other events, 126.4 us)
